TPU v7x, 32 devices: a whole 2x2x4 slice. The times are simulated.
32 devices in a mesh: groups: 2 (over y), seq: 4 (over z), tensor: 2 (over x), dp: 2 (over core).
Axes of the slice: x: 2, y: 2, z: 4, core: 2. Of those that a mesh axis runs over, the one named last changes fastest.
Arguments:
- tokens: bfloat16 [4, 1024, 4096], P(('groups', 'dp'), 'seq', 'tensor'), parts along dimension 0, may hold values from -6 to 6
- doc_lengths: int32 [4, 8], P(('groups', 'dp')), parts along dimension 0, may hold values from 1 to 768, 1024 in all within a row
- low_taps: float32 [2, 4096], P(None, 'tensor'), may hold values from 0.66 to 0.75
- high_taps: float32 [2, 4096], P(None, 'tensor'), may hold values from -2.5 to 2.5
- level_weights: float32 [13, 4096], P(None, 'tensor'), may hold values from -2.5 to 2.5
- mix_weight: bfloat16 [4096, 4096], P(None, 'tensor'), may hold values from -0.09375 to 0.09375
- out_grad: bfloat16 [4, 1024, 4096], P(('groups', 'dp'), 'seq', 'tensor'), parts along dimension 0, may hold values from -6 to 6
Outputs:
- result: bfloat16 [4, 1024, 4096], P(('groups', 'dp'), 'seq', 'tensor'), parts along dimension 0
- token_grad: bfloat16 [4, 1024, 4096], P(('groups', 'dp'), 'seq', 'tensor'), parts along dimension 0
- weight_grad: bfloat16 [8192, 4096], P(('groups', 'seq', 'dp'), 'tensor'), parts along dimension 0
- low_grad: float32 [4, 4096], P('groups', 'tensor'), parts along dimension 0
- high_grad: float32 [4, 4096], P('groups', 'tensor'), parts along dimension 0
- level_grad: float32 [26, 4096], P('groups', 'tensor'), parts along dimension 0
There are 2 independent parts, one for each index of `groups`. A program takes and returns all parts, laid end to end along the dimension named above; an argument that names none is the same for every part. Nothing has to cross between parts.
Inputs may be any that keep to these rules, and one draw needn't show every extreme that they name: `doc_lengths`: each row of 8 lengths sums to 1024, and its longest document has exactly 768 positions.
All inputs are finite; a program needn't handle non-finite values.
Results may differ from a plain program's by a relative error of at most 0.015.
Values may be sent and summed in bfloat16 or wider, within the bound.
No kernel may reach another device: no remote copies, remote signals or barrier semaphores. Data moves between devices by JAX's collectives and lax.ppermute only.
A program may use at most 128 MiB of HBM per device.

v0:
```python
import jax
import jax.numpy as jnp
from jax import lax
from jax.sharding import PartitionSpec as P

GELU_SCALE = 0.7978845608028654
GELU_CUBIC = 0.044715


def shifted_2(block, axis, distance):
    devices = range(lax.axis_size(axis))
    route = [(i - distance, i) for i in devices if i - distance in devices]
    return lax.ppermute(block, axis, route)


def gelu_value(values):
    tangent = jnp.tanh(GELU_SCALE * (values + GELU_CUBIC * values * values * values))
    return 0.5 * values * (1.0 + tangent)


def gelu_slope(values):
    tangent = jnp.tanh(GELU_SCALE * (values + GELU_CUBIC * values * values * values))
    return 0.5 * (1.0 + tangent) + 0.5 * values * (1.0 - tangent * tangent) * GELU_SCALE * (
        1.0 + 3.0 * GELU_CUBIC * values * values
    )


def doc_starts(positions, doc_lengths):
    bounds = jnp.cumsum(doc_lengths, axis=1) - doc_lengths
    before = bounds[:, None, :] <= positions[None, :, None]
    return jnp.max(jnp.where(before, bounds[:, None, :], -1), axis=2)


def tap_mask(positions, starts, spacing):
    return (positions[None, :] - spacing >= starts)[:, :, None]


def shards(tokens, doc_lengths, low_taps, high_taps, level_weights, mix_weight, out_grad):
    batch_size, row_count, channels = tokens.shape
    levels = level_weights.shape[0] - 1
    seq_count = lax.axis_size("seq")
    core_count = lax.axis_size("dp")
    grad_scale = float(batch_size * row_count * seq_count * core_count) ** (-0.5)
    offset = lax.axis_index("seq") * row_count
    positions = offset + jnp.arange(row_count, dtype=jnp.int32)
    starts = doc_starts(positions, doc_lengths)
    shallow = min(levels, row_count.bit_length() - 1)
    summed = jnp.zeros(tokens.shape, jnp.float32)
    states = [tokens]
    previous_list = []
    current = tokens
    for level_index in range(shallow):
        spacing = 2**level_index
        border = shifted_2(current[:, row_count - spacing :, :], "seq", 1)
        shifted = jnp.concatenate([border, current[:, : row_count - spacing, :]], axis=1)
        previous = jnp.where(tap_mask(positions, starts, spacing), shifted, jnp.zeros_like(shifted))
        summed = summed + level_weights[level_index] * (
            high_taps[0] * previous + high_taps[1] * current
        )
        current = (low_taps[0] * previous + low_taps[1] * current).astype(jnp.bfloat16)
        previous_list.append(previous)
        states.append(current)
    for level_index in range(shallow, levels):
        spacing = 2**level_index
        device_hops = spacing // row_count
        if device_hops < seq_count:
            shifted = shifted_2(current, "seq", device_hops)
        else:
            shifted = jnp.zeros_like(current)
        previous = jnp.where(tap_mask(positions, starts, spacing), shifted, jnp.zeros_like(shifted))
        summed = summed + level_weights[level_index] * (
            high_taps[0] * previous + high_taps[1] * current
        )
        current = (low_taps[0] * previous + low_taps[1] * current).astype(jnp.bfloat16)
        previous_list.append(previous)
        states.append(current)
    summed = summed + level_weights[levels] * current
    activated = gelu_value(summed).astype(jnp.bfloat16)
    partial_mix = jnp.einsum(
        "brc,oc->bro", activated, mix_weight, preferred_element_type=jnp.float32
    )
    mixed = lax.psum_scatter(
        partial_mix.astype(jnp.bfloat16), "tensor", scatter_dimension=2, tiled=True
    ).astype(jnp.float32)
    result = (tokens.astype(jnp.float32) + mixed).astype(jnp.bfloat16)
    gathered = lax.all_gather(out_grad, "tensor", axis=2, tiled=True)
    act_grad = jnp.einsum("bro,oc->brc", gathered, mix_weight, preferred_element_type=jnp.float32)
    weight_grad = lax.psum_scatter(
        (
            jnp.einsum("bro,brc->oc", gathered, activated, preferred_element_type=jnp.float32)
            * grad_scale
        ).astype(jnp.bfloat16),
        ("seq", "dp"),
        scatter_dimension=0,
        tiled=True,
    )
    summed_grad = act_grad * gelu_slope(summed)
    carry_grad = (level_weights[levels] * summed_grad).astype(jnp.bfloat16)
    weight_sums = [None] * (levels + 1)
    weight_sums[levels] = jnp.sum(summed_grad * states[levels].astype(jnp.float32), axis=(0, 1))
    low_first = jnp.zeros((channels,), jnp.float32)
    low_second = jnp.zeros((channels,), jnp.float32)
    high_first = jnp.zeros((channels,), jnp.float32)
    high_second = jnp.zeros((channels,), jnp.float32)
    for level_index in range(levels - 1, -1, -1):
        spacing = 2**level_index
        current = states[level_index]
        previous = previous_list[level_index]
        weighted = level_weights[level_index] * summed_grad
        highpass = high_taps[0] * previous + high_taps[1] * current
        weight_sums[level_index] = jnp.sum(summed_grad * highpass, axis=(0, 1))
        grad_wide = carry_grad.astype(jnp.float32)
        low_first = low_first + jnp.sum(grad_wide * previous.astype(jnp.float32), axis=(0, 1))
        low_second = low_second + jnp.sum(grad_wide * current.astype(jnp.float32), axis=(0, 1))
        high_first = high_first + jnp.sum(weighted * previous.astype(jnp.float32), axis=(0, 1))
        high_second = high_second + jnp.sum(weighted * current.astype(jnp.float32), axis=(0, 1))
        carried = low_taps[0] * carry_grad + high_taps[0] * weighted
        stayed = low_taps[1] * carry_grad + high_taps[1] * weighted
        outgoing = jnp.where(
            tap_mask(positions, starts, spacing), carried, jnp.zeros_like(carried)
        ).astype(jnp.bfloat16)
        if level_index < shallow:
            border = shifted_2(outgoing[:, :spacing, :], "seq", -1)
            pulled = jnp.concatenate([outgoing[:, spacing:, :], border], axis=1)
        else:
            device_hops = spacing // row_count
            if device_hops < seq_count:
                pulled = shifted_2(outgoing, "seq", -device_hops)
            else:
                pulled = jnp.zeros_like(outgoing)
        carry_grad = (stayed + pulled).astype(jnp.bfloat16)
    token_grad = (out_grad.astype(jnp.float32) + carry_grad.astype(jnp.float32)).astype(
        jnp.bfloat16
    )
    low_grad = jnp.stack([low_first, low_second]) * grad_scale
    high_grad = jnp.stack([high_first, high_second]) * grad_scale
    level_grad = jnp.stack(weight_sums) * grad_scale
    low_grad, high_grad, level_grad = (
        lax.psum(low_grad.astype(jnp.bfloat16), ("seq", "dp")).astype(jnp.float32),
        lax.psum(high_grad.astype(jnp.bfloat16), ("seq", "dp")).astype(jnp.float32),
        lax.psum(level_grad.astype(jnp.bfloat16), ("seq", "dp")).astype(jnp.float32),
    )
    return (result, token_grad, weight_grad, low_grad, high_grad, level_grad)


def solution(mesh):
    placed = (
        P(("groups", "dp"), "seq", "tensor"),
        P(("groups", "dp"), None),
        P(None, "tensor"),
        P(None, "tensor"),
        P(None, "tensor"),
        P(None, "tensor"),
        P(("groups", "dp"), "seq", "tensor"),
    )
    return jax.shard_map(
        shards,
        mesh=mesh,
        in_specs=placed,
        out_specs=(
            P(("groups", "dp"), "seq", "tensor"),
            P(("groups", "dp"), "seq", "tensor"),
            P(("groups", "seq", "dp"), "tensor"),
            P("groups", "tensor"),
            P("groups", "tensor"),
            P("groups", "tensor"),
        ),
        check_vma=False,
    )
```

profile of v0, /device:TPU:0, one launch (start us, length us, event | category | flops | bytes accessed | tf_op | source)
XLA Modules:
  0.0 566.0 jit_solution(1448448901782919432)
XLA Ops:
  8.0 4.9 collective-permute-start
  16.0 2.2 fusion.18
  18.3 3.5 collective-permute-start.1
  21.8 1.3 collective-permute-done.1
  23.9 4.2 collective-permute-start.2
  28.1 1.4 collective-permute-done.2
  30.2 4.2 collective-permute-start.3
  34.5 1.5 collective-permute-done.3
  36.7 4.2 collective-permute-start.4
  41.0 1.8 collective-permute-done.4
  43.4 4.3 collective-permute-start.5
  47.7 3.5 collective-permute-done.5
  51.8 4.4 collective-permute-start.6
  56.3 6.0 %collective-permute-done.6 = bf16[1,64,2048]{2,1,0:T(8,128)(2,1)S(1)} collective-permute-done((bf16[1,64,2048]{2,1,0:T(8,128)(2,1)S(1)}, bf16[1,64,2048]{2,1,0:T(8,128)(2,1)S(1)}, u32[]{:S(2)}, u32[]{:S(2)}) %collective-permute-start.6) | collective-permute-done | bytes 262176 | tf_op jit(solution)/shard_map/ppermute | solution.py:13
  63.0 4.4 collective-permute-start.7
  67.4 8.8 %collective-permute-done.7 = bf16[1,128,2048]{2,1,0:T(8,128)(2,1)S(1)} collective-permute-done((bf16[1,128,2048]{2,1,0:T(8,128)(2,1)S(1)}, bf16[1,128,2048]{2,1,0:T(8,128)(2,1)S(1)}, u32[]{:S(2)}, u32[]{:S(2)}) %collective-permute-start.7) | collective-permute-done | bytes 524320 | tf_op jit(solution)/shard_map/ppermute | solution.py:13
  76.2 1.5 fusion.52
  77.7 5.5 collective-permute-start.8
  83.5 14.6 %collective-permute-done.8 = bf16[1,256,2048]{2,1,0:T(8,128)(2,1)} collective-permute-done((bf16[1,256,2048]{2,1,0:T(8,128)(2,1)}, bf16[1,256,2048]{2,1,0:T(8,128)(2,1)}, u32[]{:S(2)}, u32[]{:S(2)}) %collective-permute-start.8) | collective-permute-done | bytes 1048608 | tf_op jit(solution)/shard_map/ppermute | solution.py:13
  98.1 2.1 fusion.57
  100.2 17.7 %collective-permute-start.9 = (bf16[1,256,2048]{2,1,0:T(8,128)(2,1)S(1)}, bf16[1,256,2048]{2,1,0:T(8,128)(2,1)S(1)}, u32[]{:S(2)}, u32[]{:S(2)}) collective-permute-start(bf16[1,256,2048]{2,1,0:T(8,128)(2,1)S(1)} %fusion.57), channel_id=1, source_target_pairs={{0,8},{4,12},{1,9},{5,13},{2,10},{6,14},{3,11},{7,15},{16,24},{20,... | collective-permute-start | bytes 3145736 | tf_op jit(solution)/shard_map/ppermute | solution.py:13
  117.8 1.7 fusion.183
  119.7 9.9 %collective-permute-done.9 = bf16[1,256,2048]{2,1,0:T(8,128)(2,1)S(1)} collective-permute-done((bf16[1,256,2048]{2,1,0:T(8,128)(2,1)S(1)}, bf16[1,256,2048]{2,1,0:T(8,128)(2,1)S(1)}, u32[]{:S(2)}, u32[]{:S(2)}) %collective-permute-start.9) | collective-permute-done | bytes 1048608 | tf_op jit(solution)/shard_map/ppermute | solution.py:13
  130.9 13.8 %fusion.3 = (f32[1,256,2048]{2,1,0:T(8,128)}, bf16[1,256,2048]{2,1,0:T(8,128)(2,1)}) fusion(bf16[1,256,2048]{2,1,0:T(8,128)(2,1)S(1)} %fusion.57, bf16[1,256,2048]{2,1,0:T(8,128)(2,1)} %fusion.52, bf16[1,256,2048]{2,1,0:T(8,128)(2,1)} %copy-done.15, bf16[1,256,2048]{2,1,0:T(8,128)(2,1)} %copy-done.13, bf16[1,256,2048]{2,1,0:T(8,128)(2,1)S(1)} %copy-done.11, ...), kind=kLoop, calls=%fused_computation.123 | loop fusion | flops 70254592 | bytes 24275456 | tf_op jit(solution)/shard_map/add | solution.py:77
  144.8 11.1 %fusion.88 = (bf16[1,256,2048]{2,1,0:T(8,128)(2,1)S(1)}, f32[1,256,2048]{2,1,0:T(8,128)S(1)}) fusion(f32[2048]{0:T(1024)} %bitcast.180, f32[2048]{0:T(1024)S(1)} %bitcast.105, f32[2048]{0:T(1024)} %bitcast.133, pred[256]{0:T(512)(128)(4,1)} %get-tuple-element.139, f32[2048]{0:T(1024)} %bitcast.177, f32[2048]{0:T(1024)} %bitcast.186, f32[2048]{0:T(1024)} %bitcast.116, ...), kind=kOutput, calls=%fused_computation.208 | convolution fusion | flops 4315414528 | bytes 24183040 | tf_op jit(solution)/shard_map/bro,oc->brc/dot_general | solution.py:87
  155.9 1.3 collective-permute-start.10
  157.2 38.8 %collective-permute-done.10 = bf16[1,256,2048]{2,1,0:T(8,128)(2,1)S(1)} collective-permute-done((bf16[1,256,2048]{2,1,0:T(8,128)(2,1)S(1)}, bf16[1,256,2048]{2,1,0:T(8,128)(2,1)S(1)}, u32[]{:S(2)}, u32[]{:S(2)}) %collective-permute-start.10) | collective-permute-done | bytes 1048608 | tf_op jit(solution)/shard_map/ppermute | solution.py:13
  196.1 8.5 %fusion.4 = (f32[2048]{0:T(1024)}, f32[2048]{0:T(1024)}, f32[2048]{0:T(1024)}, f32[2048]{0:T(1024)}, f32[2048]{0:T(1024)}, /*index=5*/f32[2048]{0:T(1024)}, f32[...) fusion(f32[1,256,2048]{2,1,0:T(8,128)S(1)} %get-tuple-element.1, ...), kind=kLoop, calls=%fused_computation.124 | loop fusion | flops 47667200 | bytes 9691648 | tf_op jit(solution)/shard_map/reduce_sum | solution.py:100
  205.1 1.3 collective-permute-start.11
  206.4 21.0 %collective-permute-done.11 = bf16[1,256,2048]{2,1,0:T(8,128)(2,1)S(1)} collective-permute-done((bf16[1,256,2048]{2,1,0:T(8,128)(2,1)S(1)}, bf16[1,256,2048]{2,1,0:T(8,128)(2,1)S(1)}, u32[]{:S(2)}, u32[]{:S(2)}) %collective-permute-start.11) | collective-permute-done | bytes 1048608 | tf_op jit(solution)/shard_map/ppermute | solution.py:13
  227.5 1.5 fusion.105
  229.6 1.6 collective-permute-start.12
  231.2 12.4 %collective-permute-done.12 = bf16[1,128,2048]{2,1,0:T(8,128)(2,1)S(1)} collective-permute-done((bf16[1,128,2048]{2,1,0:T(8,128)(2,1)S(1)}, bf16[1,128,2048]{2,1,0:T(8,128)(2,1)S(1)}, u32[]{:S(2)}, u32[]{:S(2)}) %collective-permute-start.12) | collective-permute-done | bytes 524320 | tf_op jit(solution)/shard_map/ppermute | solution.py:13
  243.7 1.5 fusion.113
  245.2 4.6 multiply_reduce_fusion.2
  249.8 1.4 collective-permute-start.13
  251.3 6.9 %collective-permute-done.13 = bf16[1,64,2048]{2,1,0:T(8,128)(2,1)S(1)} collective-permute-done((bf16[1,64,2048]{2,1,0:T(8,128)(2,1)S(1)}, bf16[1,64,2048]{2,1,0:T(8,128)(2,1)S(1)}, u32[]{:S(2)}, u32[]{:S(2)}) %collective-permute-start.13) | collective-permute-done | bytes 262176 | tf_op jit(solution)/shard_map/ppermute | solution.py:13
  258.2 1.5 fusion.121
  263.0 12.5 %fusion.1 = bf16[1,256,4096]{2,1,0:T(8,128)(2,1)} fusion(bf16[4096,2048]{1,0:T(8,128)(2,1)} %param.12, f32[1,256,2048]{2,1,0:T(8,128)} %get-tuple-element.111), kind=kOutput, calls=%fused_computation.3 | convolution fusion | flops 4300734464 | bytes 20971520 | tf_op jit(solution)/shard_map/brc,oc->bro/dot_general | solution.py:79
  275.7 1.3 slice.165
  277.2 2.3 fusion.129
  279.6 3.8 multiply_reduce_fusion.4
  283.4 1.4 collective-permute-start.15
  284.9 5.4 collective-permute-done.15
  291.8 1.3 collective-permute-start.16
  293.2 4.4 collective-permute-done.16
  298.6 4.1 multiply_reduce_fusion.6
  302.7 1.4 collective-permute-start.17
  304.4 4.1 collective-permute-done.17
  310.1 1.7 collective-permute-start.18
  312.1 3.7 collective-permute-done.18
  315.8 2.0 fusion.161
  318.2 7.1 %multiply_reduce_fusion.8 = (f32[2048]{0:T(1024)}, f32[2048]{0:T(1024)}, f32[2048]{0:T(1024)}, f32[2048]{0:T(1024)}, f32[2048]{0:T(1024)}, /*index=5*/f32[2048]{...) fusion(f32[1,256,2048]{2,1,0:T(8,128)S(1)} %get-tuple-element.150, ...), kind=kLoop, calls=%fused_computation.295 | loop fusion | flops 25149440 | bytes 11641344 | tf_op jit(solution)/shard_map/reduce_sum | solution.py:111
  325.4 1.7 stack.67
  331.5 13.1 %fusion = bf16[4096,2048]{0,1:T(8,128)(2,1)} fusion(bf16[1,256,4096]{2,1,0:T(8,128)(2,1)} %all-gather.2.cloned.1.call-done, f32[1,256,2048]{2,1,0:T(8,128)} %get-tuple-element.111), kind=kOutput, calls=%fused_computation.1 | convolution fusion | flops 4316463104 | bytes 20971520 | tf_op jit(solution)/shard_map/bro,brc->oc/dot_general | solution.py:90
  345.8 1.3 collective-permute-start.19
  347.3 4.0 collective-permute-done.19
  351.4 1.7 add_convert_fusion
  353.1 28.3 %all-reduce.3.cloned.1.call-done = (bf16[2,2048]{1,0:T(2,128)(2,1)}, bf16[2,2048]{1,0:T(2,128)(2,1)}, bf16[13,2048]{1,0:T(8,128)(2,1)}) async-done(((bf16[2,2048]{1,0:T(2,128)(2,1)}, bf16[2,2048]{1,0:T(2,128)(2,1)}, bf16[13,2048]{1,0:T(8,128)(2,1)}), (bf16[2,2048]{1,0:T(2,128)(2,1)}, bf16[2,2048]{1,0:T(2,128)(2,1)}, bf16[13,2048]{1,0:T(8,128)(2,1)})) %all-reduce.3.cloned.1.call-update) | async-done | bytes 69648 | tf_op jit(solution)/shard_map/psum | solution.py:139
  381.4 1.3 convert_element_type.712
  382.7 1.3 convert_element_type.714
  384.0 1.5 convert_element_type.716
  385.5 169.5 %reduce-scatter.5.cloned.1.call-done = bf16[512,2048]{0,1:T(8,128)(2,1)} async-done(((bf16[4096,2048]{0,1:T(8,128)(2,1)}), bf16[512,2048]{0,1:T(8,128)(2,1)}) %reduce-scatter.5.cloned.1.call-update) | async-done | bytes 2097168 | tf_op jit(solution)/shard_map/reduce_scatter | solution.py:88
  555.1 3.9 copy.14
  (380 shorter events, 24.5 us)
Async XLA Ops:
  7.2 137.5 %all-gather.2.cloned.1.call-start = ((), (), s32[]{:S(2)}) async-start(), calls=%async_computation.3 | async-start | bytes 3145728 | tf_op jit(solution)/shard_map/all_gather | solution.py:86
  8.0 8.0 %collective-permute-start = (bf16[1,1,2048]{2,1,0:T(2,128)(2,1)S(1)}, bf16[1,1,2048]{2,1,0:T(2,128)(2,1)S(1)}, u32[]{:S(2)}, u32[]{:S(2)}) collective-permute-start(bf16[1,1,2048]{2,1,0:T(2,128)(2,1)S(1)} %slice.100), channel_id=1, source_target_pairs={{0,4},{4,8},{8,12},{1,5},{5,9},{9,13},{2,6},{6,10},{10,14},{3,7},{... | collective-permute-start | bytes 12296 | tf_op jit(solution)/shard_map/ppermute | solution.py:13
  15.9 26.8 %copy-start.143 = (pred[256]{0:T(512)(128)(4,1)}, pred[256]{0:T(512)(128)(4,1)S(1)}, u32[]{:S(2)}) copy-start(pred[256]{0:T(512)(128)(4,1)S(1)} %get-tuple-element.144) | copy-start | bytes 772
  16.0 35.3 %copy-start.129 = (pred[256]{0:T(512)(128)(4,1)}, pred[256]{0:T(512)(128)(4,1)S(1)}, u32[]{:S(2)}) copy-start(pred[256]{0:T(512)(128)(4,1)S(1)} %get-tuple-element.143) | copy-start | bytes 772
  16.0 46.3 %copy-start.146 = (pred[256]{0:T(512)(128)(4,1)}, pred[256]{0:T(512)(128)(4,1)S(1)}, u32[]{:S(2)}) copy-start(pred[256]{0:T(512)(128)(4,1)S(1)} %get-tuple-element.142) | copy-start | bytes 772
  16.0 60.2 %copy-start.133 = (pred[256]{0:T(512)(128)(4,1)}, pred[256]{0:T(512)(128)(4,1)S(1)}, u32[]{:S(2)}) copy-start(pred[256]{0:T(512)(128)(4,1)S(1)} %get-tuple-element.141) | copy-start | bytes 772
  18.3 111.4 %copy-start = (bf16[1,256,2048]{2,1,0:T(8,128)(2,1)}, bf16[1,256,2048]{2,1,0:T(8,128)(2,1)S(1)}, u32[]{:S(2)}) copy-start(bf16[1,256,2048]{2,1,0:T(8,128)(2,1)S(1)} %fusion.18) | copy-start | bytes 3145732
  18.3 4.8 collective-permute-start.1
  23.9 5.6 collective-permute-start.2
  30.2 5.8 %collective-permute-start.3 = (bf16[1,8,2048]{2,1,0:T(8,128)(2,1)S(1)}, bf16[1,8,2048]{2,1,0:T(8,128)(2,1)S(1)}, u32[]{:S(2)}, u32[]{:S(2)}) collective-permute-start(bf16[1,8,2048]{2,1,0:T(8,128)(2,1)S(1)} %slice.151), channel_id=1, source_target_pairs={{0,4},{4,8},{8,12},{1,5},{5,9},{9,13},{2,6},{6,10},{10,14},{3,7},{... | collective-permute-start | bytes 98312 | tf_op jit(solution)/shard_map/ppermute | solution.py:13
  36.7 6.1 %collective-permute-start.4 = (bf16[1,16,2048]{2,1,0:T(8,128)(2,1)S(1)}, bf16[1,16,2048]{2,1,0:T(8,128)(2,1)S(1)}, u32[]{:S(2)}, u32[]{:S(2)}) collective-permute-start(bf16[1,16,2048]{2,1,0:T(8,128)(2,1)S(1)} %slice.153), channel_id=1, source_target_pairs={{0,4},{4,8},{8,12},{1,5},{5,9},{9,13},{2,6},{6,10},{10,14},{3,7},{... | collective-permute-start | bytes 196616 | tf_op jit(solution)/shard_map/ppermute | solution.py:13
  43.4 7.8 %collective-permute-start.5 = (bf16[1,32,2048]{2,1,0:T(8,128)(2,1)S(1)}, bf16[1,32,2048]{2,1,0:T(8,128)(2,1)S(1)}, u32[]{:S(2)}, u32[]{:S(2)}) collective-permute-start(bf16[1,32,2048]{2,1,0:T(8,128)(2,1)S(1)} %slice.155), channel_id=1, source_target_pairs={{0,4},{4,8},{8,12},{1,5},{5,9},{9,13},{2,6},{6,10},{10,14},{3,7},{... | collective-permute-start | bytes 393224 | tf_op jit(solution)/shard_map/ppermute | solution.py:13
  51.8 10.5 %collective-permute-start.6 = (bf16[1,64,2048]{2,1,0:T(8,128)(2,1)S(1)}, bf16[1,64,2048]{2,1,0:T(8,128)(2,1)S(1)}, u32[]{:S(2)}, u32[]{:S(2)}) collective-permute-start(bf16[1,64,2048]{2,1,0:T(8,128)(2,1)S(1)} %slice.157), channel_id=1, source_target_pairs={{0,4},{4,8},{8,12},{1,5},{5,9},{9,13},{2,6},{6,10},{10,14},{3,7},{... | collective-permute-start | bytes 786440 | tf_op jit(solution)/shard_map/ppermute | solution.py:13
  63.0 13.2 %collective-permute-start.7 = (bf16[1,128,2048]{2,1,0:T(8,128)(2,1)S(1)}, bf16[1,128,2048]{2,1,0:T(8,128)(2,1)S(1)}, u32[]{:S(2)}, u32[]{:S(2)}) collective-permute-start(bf16[1,128,2048]{2,1,0:T(8,128)(2,1)S(1)} %get-tuple-element.120), channel_id=1, source_target_pairs={{0,4},{4,8},{8,12},{1,5},{5,9},{9,13},{2,6},{6,10},{10,14},{3,7},{... | collective-permute-start | bytes 1572872 | tf_op jit(solution)/shard_map/ppermute | solution.py:13
  77.7 53.0 %copy-start.2 = (bf16[1,256,2048]{2,1,0:T(8,128)(2,1)S(1)}, bf16[1,256,2048]{2,1,0:T(8,128)(2,1)}, u32[]{:S(2)}) copy-start(bf16[1,256,2048]{2,1,0:T(8,128)(2,1)} %param.7) | copy-start | bytes 3145732
  77.7 20.4 %collective-permute-start.8 = (bf16[1,256,2048]{2,1,0:T(8,128)(2,1)}, bf16[1,256,2048]{2,1,0:T(8,128)(2,1)}, u32[]{:S(2)}, u32[]{:S(2)}) collective-permute-start(bf16[1,256,2048]{2,1,0:T(8,128)(2,1)} %fusion.52), channel_id=1, source_target_pairs={{0,4},{4,8},{8,12},{1,5},{5,9},{9,13},{2,6},{6,10},{10,14},{3,7},{... | collective-permute-start | bytes 3145736 | tf_op jit(solution)/shard_map/ppermute | solution.py:13
  83.2 234.7 %reduce-scatter.3.cloned.1.call-start = ((), (), s32[]{:S(2)}) async-start(), calls=%async_computation.2 | async-start | bytes 3145728 | tf_op jit(solution)/shard_map/reduce_scatter | solution.py:82
  83.3 36.2 %copy-start.139 = (f32[2,2048]{1,0:T(2,128)S(1)}, f32[2,2048]{1,0:T(2,128)}, u32[]{:S(2)}) copy-start(f32[2,2048]{1,0:T(2,128)} %param.10) | copy-start | bytes 49156
  83.3 47.4 %copy-start.5 = (bf16[1,256,2048]{2,1,0:T(8,128)(2,1)S(1)}, bf16[1,256,2048]{2,1,0:T(8,128)(2,1)}, u32[]{:S(2)}) copy-start(bf16[1,256,2048]{2,1,0:T(8,128)(2,1)} %copy-done.4) | copy-start | bytes 3145732
  83.3 47.4 %copy-start.8 = (bf16[1,256,2048]{2,1,0:T(8,128)(2,1)S(1)}, bf16[1,256,2048]{2,1,0:T(8,128)(2,1)}, u32[]{:S(2)}) copy-start(bf16[1,256,2048]{2,1,0:T(8,128)(2,1)} %copy-done.7) | copy-start | bytes 3145732
  83.3 47.4 %copy-start.11 = (bf16[1,256,2048]{2,1,0:T(8,128)(2,1)S(1)}, bf16[1,256,2048]{2,1,0:T(8,128)(2,1)}, u32[]{:S(2)}) copy-start(bf16[1,256,2048]{2,1,0:T(8,128)(2,1)} %copy-done.10) | copy-start | bytes 3145732
  83.3 47.4 %copy-start.49 = (bf16[1,16,2048]{2,1,0:T(8,128)(2,1)S(1)}, bf16[1,16,2048]{2,1,0:T(8,128)(2,1)}, u32[]{:S(2)}) copy-start(bf16[1,16,2048]{2,1,0:T(8,128)(2,1)} %copy-done.48) | copy-start | bytes 196612
  83.3 47.4 %copy-start.52 = (bf16[1,8,2048]{2,1,0:T(8,128)(2,1)S(1)}, bf16[1,8,2048]{2,1,0:T(8,128)(2,1)}, u32[]{:S(2)}) copy-start(bf16[1,8,2048]{2,1,0:T(8,128)(2,1)} %copy-done.51) | copy-start | bytes 98308
  83.4 47.4 %copy-start.55 = (bf16[1,4,2048]{2,1,0:T(4,128)(2,1)S(1)}, bf16[1,4,2048]{2,1,0:T(4,128)(2,1)}, u32[]{:S(2)}) copy-start(bf16[1,4,2048]{2,1,0:T(4,128)(2,1)} %copy-done.54) | copy-start | bytes 49156
  83.4 47.4 %copy-start.69 = (bf16[1,1,2048]{2,1,0:T(2,128)(2,1)S(1)}, bf16[1,1,2048]{2,1,0:T(2,128)(2,1)}, u32[]{:S(2)}) copy-start(bf16[1,1,2048]{2,1,0:T(2,128)(2,1)} %copy-done.68) | copy-start | bytes 12292
  83.4 47.4 %copy-start.72 = (bf16[1,2,2048]{2,1,0:T(2,128)(2,1)S(1)}, bf16[1,2,2048]{2,1,0:T(2,128)(2,1)}, u32[]{:S(2)}) copy-start(bf16[1,2,2048]{2,1,0:T(2,128)(2,1)} %copy-done.71) | copy-start | bytes 24580
  83.4 47.4 %copy-start.127 = (pred[256]{0:T(512)(128)(4,1)S(1)}, pred[256]{0:T(512)(128)(4,1)}, u32[]{:S(2)}) copy-start(pred[256]{0:T(512)(128)(4,1)} %copy-done.126) | copy-start | bytes 772
  83.4 47.4 %copy-start.130 = (pred[256]{0:T(512)(128)(4,1)S(1)}, pred[256]{0:T(512)(128)(4,1)}, u32[]{:S(2)}) copy-start(pred[256]{0:T(512)(128)(4,1)} %copy-done.129) | copy-start | bytes 772
  83.4 47.4 %copy-start.134 = (pred[256]{0:T(512)(128)(4,1)S(1)}, pred[256]{0:T(512)(128)(4,1)}, u32[]{:S(2)}) copy-start(pred[256]{0:T(512)(128)(4,1)} %copy-done.133) | copy-start | bytes 772
  83.4 47.4 %copy-start.137 = (pred[256]{0:T(512)(128)(4,1)S(1)}, pred[256]{0:T(512)(128)(4,1)}, u32[]{:S(2)}) copy-start(pred[256]{0:T(512)(128)(4,1)} %copy-done.136) | copy-start | bytes 772
  83.4 47.4 %copy-start.141 = (pred[256]{0:T(512)(128)(4,1)S(1)}, pred[256]{0:T(512)(128)(4,1)}, u32[]{:S(2)}) copy-start(pred[256]{0:T(512)(128)(4,1)} %copy-done.140) | copy-start | bytes 772
  83.4 47.4 %copy-start.144 = (pred[256]{0:T(512)(128)(4,1)S(1)}, pred[256]{0:T(512)(128)(4,1)}, u32[]{:S(2)}) copy-start(pred[256]{0:T(512)(128)(4,1)} %copy-done.143) | copy-start | bytes 772
  83.4 47.4 %copy-start.147 = (pred[256]{0:T(512)(128)(4,1)S(1)}, pred[256]{0:T(512)(128)(4,1)}, u32[]{:S(2)}) copy-start(pred[256]{0:T(512)(128)(4,1)} %copy-done.146) | copy-start | bytes 772
  83.5 47.4 %copy-start.149 = (pred[256]{0:T(512)(128)(4,1)S(1)}, pred[256]{0:T(512)(128)(4,1)}, u32[]{:S(2)}) copy-start(pred[256]{0:T(512)(128)(4,1)} %get-tuple-element.140) | copy-start | bytes 772
  83.5 47.4 %copy-start.152 = (pred[256]{0:T(512)(128)(4,1)S(1)}, pred[256]{0:T(512)(128)(4,1)}, u32[]{:S(2)}) copy-start(pred[256]{0:T(512)(128)(4,1)} %copy-done.151) | copy-start | bytes 772
  83.5 47.4 %copy-start.154 = (pred[256]{0:T(512)(128)(4,1)S(1)}, pred[256]{0:T(512)(128)(4,1)}, u32[]{:S(2)}) copy-start(pred[256]{0:T(512)(128)(4,1)} %get-tuple-element.139) | copy-start | bytes 772
  100.2 29.5 %copy-start.31 = (bf16[1,256,2048]{2,1,0:T(8,128)(2,1)}, bf16[1,256,2048]{2,1,0:T(8,128)(2,1)S(1)}, u32[]{:S(2)}) copy-start(bf16[1,256,2048]{2,1,0:T(8,128)(2,1)S(1)} %fusion.57) | copy-start | bytes 3145732
  100.2 29.5 %collective-permute-start.9 = (bf16[1,256,2048]{2,1,0:T(8,128)(2,1)S(1)}, bf16[1,256,2048]{2,1,0:T(8,128)(2,1)S(1)}, u32[]{:S(2)}, u32[]{:S(2)}) collective-permute-start(bf16[1,256,2048]{2,1,0:T(8,128)(2,1)S(1)} %fusion.57), channel_id=1, source_target_pairs={{0,8},{4,12},{1,9},{5,13},{2,10},{6,14},{3,11},{7,15},{16,24},{20,... | collective-permute-start | bytes 3145736 | tf_op jit(solution)/shard_map/ppermute | solution.py:13
  144.6 51.4 %copy-start.32 = (bf16[1,256,2048]{2,1,0:T(8,128)(2,1)S(1)}, bf16[1,256,2048]{2,1,0:T(8,128)(2,1)}, u32[]{:S(2)}) copy-start(bf16[1,256,2048]{2,1,0:T(8,128)(2,1)} %copy-done.31) | copy-start | bytes 3145732
  144.7 51.4 %copy-start.38 = (bf16[1,256,2048]{2,1,0:T(8,128)(2,1)S(1)}, bf16[1,256,2048]{2,1,0:T(8,128)(2,1)}, u32[]{:S(2)}) copy-start(bf16[1,256,2048]{2,1,0:T(8,128)(2,1)} %copy-done.37) | copy-start | bytes 3145732
  144.7 51.4 %copy-start.39 = (bf16[1,256,2048]{2,1,0:T(8,128)(2,1)S(1)}, bf16[1,256,2048]{2,1,0:T(8,128)(2,1)}, u32[]{:S(2)}) copy-start(bf16[1,256,2048]{2,1,0:T(8,128)(2,1)} %get-tuple-element.112) | copy-start | bytes 3145732
  144.7 51.3 %copy-start.43 = (f32[1,2048]{1,0:T(1,128)S(1)}, f32[1,2048]{1,0:T(1,128)}, u32[]{:S(2)}) copy-start(f32[1,2048]{1,0:T(1,128)} %copy-done.42) | copy-start | bytes 24580
  144.7 51.3 %copy-start.46 = (f32[1,2048]{1,0:T(1,128)S(1)}, f32[1,2048]{1,0:T(1,128)}, u32[]{:S(2)}) copy-start(f32[1,2048]{1,0:T(1,128)} %copy-done.45) | copy-start | bytes 24580
  144.7 51.3 %copy-start.67 = (f32[1,2048]{1,0:T(1,128)S(1)}, f32[1,2048]{1,0:T(1,128)}, u32[]{:S(2)}) copy-start(f32[1,2048]{1,0:T(1,128)} %copy-done.66) | copy-start | bytes 24580
  144.7 51.3 %copy-start.83 = (f32[2048]{0:T(1024)S(1)}, f32[2048]{0:T(1024)}, u32[]{:S(2)}) copy-start(f32[2048]{0:T(1024)} %copy-done.82) | copy-start | bytes 24580
  144.7 51.3 %copy-start.85 = (f32[2048]{0:T(1024)S(1)}, f32[2048]{0:T(1024)}, u32[]{:S(2)}) copy-start(f32[2048]{0:T(1024)} %copy-done.84) | copy-start | bytes 24580
  144.7 51.3 %copy-start.87 = (f32[1,2048]{1,0:T(1,128)S(1)}, f32[1,2048]{1,0:T(1,128)}, u32[]{:S(2)}) copy-start(f32[1,2048]{1,0:T(1,128)} %copy-done.86) | copy-start | bytes 24580
  144.7 51.3 %copy-start.89 = (f32[1,2048]{1,0:T(1,128)S(1)}, f32[1,2048]{1,0:T(1,128)}, u32[]{:S(2)}) copy-start(f32[1,2048]{1,0:T(1,128)} %copy-done.88) | copy-start | bytes 24580
  144.8 51.3 %copy-start.91 = (f32[1,2048]{1,0:T(1,128)S(1)}, f32[1,2048]{1,0:T(1,128)}, u32[]{:S(2)}) copy-start(f32[1,2048]{1,0:T(1,128)} %copy-done.90) | copy-start | bytes 24580
  144.8 51.3 %copy-start.93 = (f32[1,2048]{1,0:T(1,128)S(1)}, f32[1,2048]{1,0:T(1,128)}, u32[]{:S(2)}) copy-start(f32[1,2048]{1,0:T(1,128)} %copy-done.92) | copy-start | bytes 24580
  144.8 51.3 %copy-start.150 = (pred[256]{0:T(512)(128)(4,1)S(1)}, pred[256]{0:T(512)(128)(4,1)}, u32[]{:S(2)}) copy-start(pred[256]{0:T(512)(128)(4,1)} %get-tuple-element.140) | copy-start | bytes 772
  144.8 51.3 %copy-start.155 = (pred[256]{0:T(512)(128)(4,1)S(1)}, pred[256]{0:T(512)(128)(4,1)}, u32[]{:S(2)}) copy-start(pred[256]{0:T(512)(128)(4,1)} %get-tuple-element.139) | copy-start | bytes 772
  155.9 40.1 %collective-permute-start.10 = (bf16[1,256,2048]{2,1,0:T(8,128)(2,1)S(1)}, bf16[1,256,2048]{2,1,0:T(8,128)(2,1)S(1)}, u32[]{:S(2)}, u32[]{:S(2)}) collective-permute-start(bf16[1,256,2048]{2,1,0:T(8,128)(2,1)S(1)} %get-tuple-element.149), channel_id=1, source_target_pairs={{8,0},{12,4},{9,1},{13,5},{10,2},{14,6},{11,3},{15,7},{24,16},{28,... | collective-permute-start | bytes 3145736 | tf_op jit(solution)/shard_map/ppermute | solution.py:13
  205.1 22.3 %collective-permute-start.11 = (bf16[1,256,2048]{2,1,0:T(8,128)(2,1)S(1)}, bf16[1,256,2048]{2,1,0:T(8,128)(2,1)S(1)}, u32[]{:S(2)}, u32[]{:S(2)}) collective-permute-start(bf16[1,256,2048]{2,1,0:T(8,128)(2,1)S(1)} %fusion.96), channel_id=1, source_target_pairs={{4,0},{8,4},{12,8},{5,1},{9,5},{13,9},{6,2},{10,6},{14,10},{7,3},{... | collective-permute-start | bytes 3145736 | tf_op jit(solution)/shard_map/ppermute | solution.py:13
  229.6 14.0 %collective-permute-start.12 = (bf16[1,128,2048]{2,1,0:T(8,128)(2,1)S(1)}, bf16[1,128,2048]{2,1,0:T(8,128)(2,1)S(1)}, u32[]{:S(2)}, u32[]{:S(2)}) collective-permute-start(bf16[1,128,2048]{2,1,0:T(8,128)(2,1)S(1)} %get-tuple-element.119), channel_id=1, source_target_pairs={{4,0},{8,4},{12,8},{5,1},{9,5},{13,9},{6,2},{10,6},{14,10},{7,3},{... | collective-permute-start | bytes 1572872 | tf_op jit(solution)/shard_map/ppermute | solution.py:13
  249.8 8.4 %collective-permute-start.13 = (bf16[1,64,2048]{2,1,0:T(8,128)(2,1)S(1)}, bf16[1,64,2048]{2,1,0:T(8,128)(2,1)S(1)}, u32[]{:S(2)}, u32[]{:S(2)}) collective-permute-start(bf16[1,64,2048]{2,1,0:T(8,128)(2,1)S(1)} %slice.164), channel_id=1, source_target_pairs={{4,0},{8,4},{12,8},{5,1},{9,5},{13,9},{6,2},{10,6},{14,10},{7,3},{... | collective-permute-start | bytes 786440 | tf_op jit(solution)/shard_map/ppermute | solution.py:13
  261.7 15.5 %collective-permute-start.14 = (bf16[1,32,2048]{2,1,0:T(8,128)(2,1)}, bf16[1,32,2048]{2,1,0:T(8,128)(2,1)S(1)}, u32[]{:S(2)}, u32[]{:S(2)}) collective-permute-start(bf16[1,32,2048]{2,1,0:T(8,128)(2,1)} %slice.166), channel_id=1, source_target_pairs={{4,0},{8,4},{12,8},{5,1},{9,5},{13,9},{6,2},{10,6},{14,10},{7,3},{... | collective-permute-start | bytes 393224 | tf_op jit(solution)/shard_map/ppermute | solution.py:13
  275.5 106.0 %all-reduce.3.cloned.1.call-start = ((), (), s32[]{:S(2)}) async-start(), calls=%async_computation.5 | async-start | bytes 163840 | tf_op jit(solution)/shard_map/psum | solution.py:139
  283.4 6.9 %collective-permute-start.15 = (bf16[1,16,2048]{2,1,0:T(8,128)(2,1)S(1)}, bf16[1,16,2048]{2,1,0:T(8,128)(2,1)S(1)}, u32[]{:S(2)}, u32[]{:S(2)}) collective-permute-start(bf16[1,16,2048]{2,1,0:T(8,128)(2,1)S(1)} %slice.168), channel_id=1, source_target_pairs={{4,0},{8,4},{12,8},{5,1},{9,5},{13,9},{6,2},{10,6},{14,10},{7,3},{... | collective-permute-start | bytes 196616 | tf_op jit(solution)/shard_map/ppermute | solution.py:13
  291.8 5.8 %collective-permute-start.16 = (bf16[1,8,2048]{2,1,0:T(8,128)(2,1)S(1)}, bf16[1,8,2048]{2,1,0:T(8,128)(2,1)S(1)}, u32[]{:S(2)}, u32[]{:S(2)}) collective-permute-start(bf16[1,8,2048]{2,1,0:T(8,128)(2,1)S(1)} %slice.170), channel_id=1, source_target_pairs={{4,0},{8,4},{12,8},{5,1},{9,5},{13,9},{6,2},{10,6},{14,10},{7,3},{... | collective-permute-start | bytes 98312 | tf_op jit(solution)/shard_map/ppermute | solution.py:13
  302.7 5.8 %collective-permute-start.17 = (bf16[1,4,2048]{2,1,0:T(4,128)(2,1)S(1)}, bf16[1,4,2048]{2,1,0:T(4,128)(2,1)S(1)}, u32[]{:S(2)}, u32[]{:S(2)}) collective-permute-start(bf16[1,4,2048]{2,1,0:T(4,128)(2,1)S(1)} %slice.172), channel_id=1, source_target_pairs={{4,0},{8,4},{12,8},{5,1},{9,5},{13,9},{6,2},{10,6},{14,10},{7,3},{... | collective-permute-start | bytes 49160 | tf_op jit(solution)/shard_map/ppermute | solution.py:13
  310.1 5.7 %collective-permute-start.18 = (bf16[1,2,2048]{2,1,0:T(2,128)(2,1)S(1)}, bf16[1,2,2048]{2,1,0:T(2,128)(2,1)S(1)}, u32[]{:S(2)}, u32[]{:S(2)}) collective-permute-start(bf16[1,2,2048]{2,1,0:T(2,128)(2,1)S(1)} %slice.348), channel_id=1, source_target_pairs={{4,0},{8,4},{12,8},{5,1},{9,5},{13,9},{6,2},{10,6},{14,10},{7,3},{... | collective-permute-start | bytes 24584 | tf_op jit(solution)/shard_map/ppermute | solution.py:13
  331.4 223.7 %reduce-scatter.5.cloned.1.call-start = ((), (), s32[]{:S(2)}) async-start(), calls=%async_computation.4 | async-start | bytes 18874368 | tf_op jit(solution)/shard_map/reduce_scatter | solution.py:88
  345.8 5.6 collective-permute-start.19
  (116 other events, 931.4 us)
Sparse Core Ops, SparseCore 0:
  83.4 32.4 all-gather.1
  275.6 32.0 reduce-scatter.2
  331.5 49.8 all-reduce.2
  383.6 171.3 reduce-scatter.4
where the time goes:
time: 573 us; the launch traced here: 566 us
  waiting for transfers between devices  347 us (61%)
  other arithmetic  77.7 us (14%)
  starting transfers between devices  71.6 us (12%)
  matrix products  36.7 us (6%)
  between operations  16.5 us (3%)
  local copies, waits for them, and re-layouts  16.1 us (3%)
    reduce_scatter x1, waiting for transfers between devices, shards(): lax.psum_scatter((jnp.einsum('bro,brc->oc', gathered, activated, preferre...  170 us
    ppermute x20, waiting for transfers between devices, shifted_2(): return lax.ppermute(block, axis, route)  149 us
    ppermute x20, starting transfers between devices, shifted_2(): return lax.ppermute(block, axis, route)  71.3 us
    psum x1, waiting for transfers between devices, shards(): lax.psum(low_grad.astype(jnp.bfloat16), ('seq', 'dp')).astype(jnp.float32)  28.3 us
    reduce_sum x4, other arithmetic, shards(): weight_sums[level_index] = jnp.sum(summed_grad * highpass, axis=(0, 1))  19.5 us
    add x1, other arithmetic, shards(): summed = summed + level_weights[levels] * current  13.8 us
    dot_general x1, matrix products, shards(): jnp.einsum('bro,brc->oc', gathered, activated, preferred_element_type=jnp...  13.1 us
    dot_general x1, matrix products, shards(): jnp.einsum('brc,oc->bro', activated, mix_weight, preferred_element_type=j...  12.5 us
  transfers between devices with their start and end apart: 24, of which 20 were waited for; matrix products, arithmetic and copies ran while one was open for 12% of the time, Pallas kernels for 0%

commit v1 on v0

--- a/solution.py
+++ b/solution.py
@@ -11,6 +11,20 @@
     devices = range(lax.axis_size(axis))
     route = [(i - distance, i) for i in devices if i - distance in devices]
     return lax.ppermute(block, axis, route)
+
+
+def exchange_sum(values, axes):
+    for axis in axes:
+        size = lax.axis_size(axis)
+        if size & (size - 1):
+            values = lax.psum(values, axis)
+            continue
+        step = 1
+        while step < size:
+            route = [(i, i ^ step) for i in range(size)]
+            values = values + lax.ppermute(values, axis, route)
+            step *= 2
+    return values
 
 
 def gelu_value(values):
@@ -85,11 +99,13 @@
     result = (tokens.astype(jnp.float32) + mixed).astype(jnp.bfloat16)
     gathered = lax.all_gather(out_grad, "tensor", axis=2, tiled=True)
     act_grad = jnp.einsum("bro,oc->brc", gathered, mix_weight, preferred_element_type=jnp.float32)
+    weight_part = (
+        jnp.einsum("bro,brc->oc", gathered, activated, preferred_element_type=jnp.float32)
+        * grad_scale
+    ).astype(jnp.bfloat16)
+    weight_part, act_grad = lax.optimization_barrier((weight_part, act_grad))
     weight_grad = lax.psum_scatter(
-        (
-            jnp.einsum("bro,brc->oc", gathered, activated, preferred_element_type=jnp.float32)
-            * grad_scale
-        ).astype(jnp.bfloat16),
+        weight_part,
         ("seq", "dp"),
         scatter_dimension=0,
         tiled=True,
@@ -135,11 +151,8 @@
     low_grad = jnp.stack([low_first, low_second]) * grad_scale
     high_grad = jnp.stack([high_first, high_second]) * grad_scale
     level_grad = jnp.stack(weight_sums) * grad_scale
-    low_grad, high_grad, level_grad = (
-        lax.psum(low_grad.astype(jnp.bfloat16), ("seq", "dp")).astype(jnp.float32),
-        lax.psum(high_grad.astype(jnp.bfloat16), ("seq", "dp")).astype(jnp.float32),
-        lax.psum(level_grad.astype(jnp.bfloat16), ("seq", "dp")).astype(jnp.float32),
-    )
+    sums = exchange_sum(jnp.concatenate([low_grad, high_grad, level_grad], axis=0), ("dp", "seq"))
+    low_grad, high_grad, level_grad = sums[0:2], sums[2:4], sums[4:]
     return (result, token_grad, weight_grad, low_grad, high_grad, level_grad)
 
 

time: 573 us -> 457 us (0.80)
  waiting for transfers between devices: 347 us -> 239 us
    reduce_scatter x1, waiting for transfers between devices: 170 us -> 0.01 us  [shards(): lax.psum_scatter(weight_part, ('seq', 'dp'), scatter_dimension=0, tiled=T...]
    ppermute x20, waiting for transfers between devices: 149 us -> 223 us  [shifted_2(): return lax.ppermute(block, axis, route)]
    psum x1 -> x0, waiting for transfers between devices: 28.3 us -> none  [shards(): lax.psum(low_grad.astype(jnp.bfloat16), ('seq', 'dp')).astype(jnp.float32)]
    ppermute x0 -> x3, waiting for transfers between devices: none -> 15.5 us  [exchange_sum(): values = values + lax.ppermute(values, axis, route)]
    convert_element_type x6 -> x0, other arithmetic: 6 us -> none  [the longest x1 1.5 us: shards(): lax.psum(level_grad.astype(jnp.bfloat16), ('seq', 'dp')).astype(jnp.float32)]
  transfers between devices with their start and end apart: 24 -> 26, of which waited for: 20 -> 21; matrix products, arithmetic and copies ran while one was open for 12% -> 24% of each run, Pallas kernels for 0% -> 0%
where the time goes in v1:
time: 457 us; the launch traced here: 450 us
  waiting for transfers between devices  239 us (52%)
  other arithmetic  73.5 us (16%)
  starting transfers between devices  72 us (16%)
  matrix products  35 us (8%)
  between operations  16.3 us (4%)
  local copies, waits for them, and re-layouts  14.2 us (3%)
    ppermute x20, waiting for transfers between devices, shifted_2(): return lax.ppermute(block, axis, route)  223 us
    ppermute x20, starting transfers between devices, shifted_2(): return lax.ppermute(block, axis, route)  71.5 us
    reduce_sum x4, other arithmetic, shards(): jnp.sum(weighted * previous.astype(jnp.float32), axis=(0, 1))  19.6 us
    ppermute x3, waiting for transfers between devices, exchange_sum(): values = values + lax.ppermute(values, axis, route)  15.5 us
    add x1, other arithmetic, shards(): summed = summed + level_weights[levels] * current  14.1 us
    dot_general x1, matrix products, shards(): jnp.einsum('brc,oc->bro', activated, mix_weight, preferred_element_type=j...  12.4 us
    dot_general x1, matrix products, shards(): jnp.einsum('bro,oc->brc', gathered, mix_weight, preferred_element_type=jn...  12.3 us
    dot_general x1, matrix products, shards(): jnp.einsum('bro,brc->oc', gathered, activated, preferred_element_type=jnp...  10.2 us
  transfers between devices with their start and end apart: 26, of which 21 were waited for; matrix products, arithmetic and copies ran while one was open for 24% of the time, Pallas kernels for 0%

profile of v1, /device:TPU:0, one launch (start us, length us, event | category | flops | bytes accessed | tf_op | source)
XLA Modules:
  0.0 449.6 jit_solution(9044396896740791133)
XLA Ops:
  8.0 4.9 %collective-permute-start = (bf16[1,1,2048]{2,1,0:T(2,128)(2,1)S(1)}, bf16[1,1,2048]{2,1,0:T(2,128)(2,1)S(1)}, u32[]{:S(2)}, u32[]{:S(2)}) collective-permute-start(bf16[1,1,2048]{2,1,0:T(2,128)(2,1)S(1)} %slice.106), channel_id=1, source_target_pairs={{0,4},{4,8},{8,12},{1,5},{5,9},{9,13},{2,6},{6,10},{10,14},{3,7},{... | collective-permute-start | bytes 12296 | tf_op jit(solution)/shard_map/ppermute | solution.py:13
  16.0 2.3 fusion.18
  18.3 3.5 collective-permute-start.1
  21.8 1.3 collective-permute-done.1
  23.9 4.2 collective-permute-start.2
  28.1 1.4 collective-permute-done.2
  30.3 4.2 collective-permute-start.3
  34.6 1.5 collective-permute-done.3
  36.6 4.2 collective-permute-start.4
  41.0 1.8 collective-permute-done.4
  43.4 4.3 collective-permute-start.5
  47.7 3.5 collective-permute-done.5
  51.9 4.4 collective-permute-start.6
  56.4 6.0 %collective-permute-done.6 = bf16[1,64,2048]{2,1,0:T(8,128)(2,1)S(1)} collective-permute-done((bf16[1,64,2048]{2,1,0:T(8,128)(2,1)S(1)}, bf16[1,64,2048]{2,1,0:T(8,128)(2,1)S(1)}, u32[]{:S(2)}, u32[]{:S(2)}) %collective-permute-start.6) | collective-permute-done | bytes 262176 | tf_op jit(solution)/shard_map/ppermute | solution.py:13
  63.2 4.4 collective-permute-start.7
  67.6 8.9 %collective-permute-done.7 = bf16[1,128,2048]{2,1,0:T(8,128)(2,1)S(1)} collective-permute-done((bf16[1,128,2048]{2,1,0:T(8,128)(2,1)S(1)}, bf16[1,128,2048]{2,1,0:T(8,128)(2,1)S(1)}, u32[]{:S(2)}, u32[]{:S(2)}) %collective-permute-start.7) | collective-permute-done | bytes 524320 | tf_op jit(solution)/shard_map/ppermute | solution.py:13
  76.5 1.5 fusion.52
  78.0 5.6 %collective-permute-start.8 = (bf16[1,256,2048]{2,1,0:T(8,128)(2,1)}, bf16[1,256,2048]{2,1,0:T(8,128)(2,1)}, u32[]{:S(2)}, u32[]{:S(2)}) collective-permute-start(bf16[1,256,2048]{2,1,0:T(8,128)(2,1)} %fusion.52), channel_id=1, source_target_pairs={{0,4},{4,8},{8,12},{1,5},{5,9},{9,13},{2,6},{6,10},{10,14},{3,7},{... | collective-permute-start | bytes 3145736 | tf_op jit(solution)/shard_map/ppermute | solution.py:13
  83.7 14.7 %collective-permute-done.8 = bf16[1,256,2048]{2,1,0:T(8,128)(2,1)} collective-permute-done((bf16[1,256,2048]{2,1,0:T(8,128)(2,1)}, bf16[1,256,2048]{2,1,0:T(8,128)(2,1)}, u32[]{:S(2)}, u32[]{:S(2)}) %collective-permute-start.8) | collective-permute-done | bytes 1048608 | tf_op jit(solution)/shard_map/ppermute | solution.py:13
  98.3 2.1 fusion.57
  100.4 17.7 %collective-permute-start.9 = (bf16[1,256,2048]{2,1,0:T(8,128)(2,1)S(1)}, bf16[1,256,2048]{2,1,0:T(8,128)(2,1)S(1)}, u32[]{:S(2)}, u32[]{:S(2)}) collective-permute-start(bf16[1,256,2048]{2,1,0:T(8,128)(2,1)S(1)} %fusion.57), channel_id=1, source_target_pairs={{0,8},{4,12},{1,9},{5,13},{2,10},{6,14},{3,11},{7,15},{16,24},{20,... | collective-permute-start | bytes 3145736 | tf_op jit(solution)/shard_map/ppermute | solution.py:13
  119.0 1.7 fusion.184
  120.8 9.1 %collective-permute-done.9 = bf16[1,256,2048]{2,1,0:T(8,128)(2,1)S(1)} collective-permute-done((bf16[1,256,2048]{2,1,0:T(8,128)(2,1)S(1)}, bf16[1,256,2048]{2,1,0:T(8,128)(2,1)S(1)}, u32[]{:S(2)}, u32[]{:S(2)}) %collective-permute-start.9) | collective-permute-done | bytes 1048608 | tf_op jit(solution)/shard_map/ppermute | solution.py:13
  130.0 14.1 %fusion.2 = (f32[1,256,2048]{2,1,0:T(8,128)}, bf16[1,256,2048]{2,1,0:T(8,128)(2,1)}) fusion(bf16[1,256,2048]{2,1,0:T(8,128)(2,1)S(1)} %fusion.57, bf16[1,256,2048]{2,1,0:T(8,128)(2,1)} %fusion.52, bf16[1,256,2048]{2,1,0:T(8,128)(2,1)S(1)} %copy-done.11, bf16[1,256,2048]{2,1,0:T(8,128)(2,1)} %copy-done.15, bf16[1,256,2048]{2,1,0:T(8,128)(2,1)S(1)} %copy-done.5, ...), kind=kLoop, calls=%fused_computation.122 | loop fusion | flops 70254592 | bytes 24275456 | tf_op jit(solution)/shard_map/add | solution.py:91
  144.3 12.4 %fusion.1 = bf16[1,256,4096]{2,1,0:T(8,128)(2,1)} fusion(bf16[4096,2048]{1,0:T(8,128)(2,1)} %param.12, f32[1,256,2048]{2,1,0:T(8,128)} %get-tuple-element.114), kind=kOutput, calls=%fused_computation.3 | convolution fusion | flops 4300734464 | bytes 20971520 | tf_op jit(solution)/shard_map/brc,oc->bro/dot_general | solution.py:93
  157.0 12.3 %convolution_bitcast_fusion = f32[1,256,2048]{2,1,0:T(8,128)} fusion(bf16[4096,2048]{1,0:T(8,128)(2,1)} %param.12, bf16[1,256,4096]{2,1,0:T(8,128)(2,1)} %all-gather.2.cloned.1.call-done), kind=kOutput, calls=%fused_computation.119 | convolution fusion | flops 4294967296 | bytes 20971520 | tf_op jit(solution)/shard_map/bro,oc->brc/dot_general | solution.py:101
  169.4 10.2 %fusion = bf16[4096,2048]{0,1:T(8,128)(2,1)} fusion(bf16[1,256,4096]{2,1,0:T(8,128)(2,1)} %all-gather.2.cloned.1.call-done, f32[1,256,2048]{2,1,0:T(8,128)S(1)} %copy-done.33), kind=kOutput, calls=%fused_computation.1 | convolution fusion | flops 4316463104 | bytes 20971520 | tf_op jit(solution)/shard_map/bro,brc->oc/dot_general | solution.py:103
  179.7 4.1 fusion.88
  183.9 1.3 collective-permute-start.10
  185.2 57.9 %collective-permute-done.10 = bf16[1,256,2048]{2,1,0:T(8,128)(2,1)S(1)} collective-permute-done((bf16[1,256,2048]{2,1,0:T(8,128)(2,1)S(1)}, bf16[1,256,2048]{2,1,0:T(8,128)(2,1)S(1)}, u32[]{:S(2)}, u32[]{:S(2)}) %collective-permute-start.10) | collective-permute-done | bytes 1048608 | tf_op jit(solution)/shard_map/ppermute | solution.py:13
  243.2 8.5 %fusion.73 = (f32[2048]{0:T(1024)}, f32[2048]{0:T(1024)}, f32[2048]{0:T(1024)}, f32[2048]{0:T(1024)}, f32[2048]{0:T(1024)}, /*index=5*/f32[2048]{0:T(1024)}, f32...) fusion(bf16[1,256,2048]{2,1,0:T(8,128)(2,1)S(1)} %copy-done.37,, ...), kind=kLoop, calls=%fused_computation.193 | loop fusion | flops 47667200 | bytes 9691648 | tf_op jit(solution)/shard_map/reduce_sum | solution.py:130
  252.2 1.3 collective-permute-start.11
  253.5 47.8 %collective-permute-done.11 = bf16[1,256,2048]{2,1,0:T(8,128)(2,1)S(1)} collective-permute-done((bf16[1,256,2048]{2,1,0:T(8,128)(2,1)S(1)}, bf16[1,256,2048]{2,1,0:T(8,128)(2,1)S(1)}, u32[]{:S(2)}, u32[]{:S(2)}) %collective-permute-start.11) | collective-permute-done | bytes 1048608 | tf_op jit(solution)/shard_map/ppermute | solution.py:13
  301.3 0.9 fusion.105
  302.9 1.6 collective-permute-start.12
  304.5 24.2 %collective-permute-done.12 = bf16[1,128,2048]{2,1,0:T(8,128)(2,1)S(1)} collective-permute-done((bf16[1,128,2048]{2,1,0:T(8,128)(2,1)S(1)}, bf16[1,128,2048]{2,1,0:T(8,128)(2,1)S(1)}, u32[]{:S(2)}, u32[]{:S(2)}) %collective-permute-start.12) | collective-permute-done | bytes 524320 | tf_op jit(solution)/shard_map/ppermute | solution.py:13
  328.8 0.9 fusion.113
  330.3 1.4 collective-permute-start.13
  331.8 14.1 %collective-permute-done.13 = bf16[1,64,2048]{2,1,0:T(8,128)(2,1)S(1)} collective-permute-done((bf16[1,64,2048]{2,1,0:T(8,128)(2,1)S(1)}, bf16[1,64,2048]{2,1,0:T(8,128)(2,1)S(1)}, u32[]{:S(2)}, u32[]{:S(2)}) %collective-permute-start.13) | collective-permute-done | bytes 262176 | tf_op jit(solution)/shard_map/ppermute | solution.py:13
  345.9 0.9 fusion.121
  347.4 1.4 collective-permute-start.14
  348.9 9.1 %collective-permute-done.14 = bf16[1,32,2048]{2,1,0:T(8,128)(2,1)S(1)} collective-permute-done((bf16[1,32,2048]{2,1,0:T(8,128)(2,1)S(1)}, bf16[1,32,2048]{2,1,0:T(8,128)(2,1)S(1)}, u32[]{:S(2)}, u32[]{:S(2)}) %collective-permute-start.14) | collective-permute-done | bytes 131104 | tf_op jit(solution)/shard_map/ppermute | solution.py:13
  359.0 4.0 fusion.38
  362.9 1.4 collective-permute-start.15
  364.5 7.1 %collective-permute-done.15 = bf16[1,16,2048]{2,1,0:T(8,128)(2,1)S(1)} collective-permute-done((bf16[1,16,2048]{2,1,0:T(8,128)(2,1)S(1)}, bf16[1,16,2048]{2,1,0:T(8,128)(2,1)S(1)}, u32[]{:S(2)}, u32[]{:S(2)}) %collective-permute-start.15) | collective-permute-done | bytes 65568 | tf_op jit(solution)/shard_map/ppermute | solution.py:13
  372.5 4.2 fusion.33
  376.8 1.5 collective-permute-start.16
  378.4 5.4 %collective-permute-done.16 = bf16[1,8,2048]{2,1,0:T(8,128)(2,1)S(1)} collective-permute-done((bf16[1,8,2048]{2,1,0:T(8,128)(2,1)S(1)}, bf16[1,8,2048]{2,1,0:T(8,128)(2,1)S(1)}, u32[]{:S(2)}, u32[]{:S(2)}) %collective-permute-start.16) | collective-permute-done | bytes 32800 | tf_op jit(solution)/shard_map/ppermute | solution.py:13
  383.8 1.0 fusion.145
  384.8 4.2 fusion.43
  389.1 1.4 collective-permute-start.17
  390.8 4.8 %collective-permute-done.17 = bf16[1,4,2048]{2,1,0:T(4,128)(2,1)S(1)} collective-permute-done((bf16[1,4,2048]{2,1,0:T(4,128)(2,1)S(1)}, bf16[1,4,2048]{2,1,0:T(4,128)(2,1)S(1)}, u32[]{:S(2)}, u32[]{:S(2)}) %collective-permute-start.17) | collective-permute-done | bytes 16416 | tf_op jit(solution)/shard_map/ppermute | solution.py:13
  395.5 1.1 fusion.153
  397.2 1.4 collective-permute-start.18
  398.9 4.4 collective-permute-done.18
  403.3 2.0 fusion.161
  405.7 7.2 %fusion.23 = (f32[2048]{0:T(1024)}, f32[2048]{0:T(1024)}, f32[2048]{0:T(1024)}, f32[2048]{0:T(1024)}, f32[2048]{0:T(1024)}, /*index=5*/f32[2048]{0:T(1024)}, f32...) fusion(f32[1,256,2048]{2,1,0:T(8,128)S(1)} %get-tuple-element.113, ...), kind=kLoop, calls=%fused_computation.143 | loop fusion | flops 25149440 | bytes 11641344 | tf_op jit(solution)/shard_map/reduce_sum | solution.py:131
  412.9 1.8 stack.67
  417.6 1.4 collective-permute-done.20
  419.9 1.3 collective-permute-start.19
  421.5 4.7 %collective-permute-done.21 = f32[17,2048]{1,0:T(8,128)S(1)} collective-permute-done((f32[17,2048]{1,0:T(8,128)S(1)}, f32[17,2048]{1,0:T(8,128)S(1)}, u32[]{:S(2)}, u32[]{:S(2)}) %collective-permute-start.21) | collective-permute-done | bytes 139296 | tf_op jit(solution)/shard_map/ppermute | solution.py:25
  426.3 1.7 add_convert_fusion
  428.1 9.4 %collective-permute-done.22 = f32[17,2048]{1,0:T(8,128)S(1)} collective-permute-done((f32[17,2048]{1,0:T(8,128)S(1)}, f32[17,2048]{1,0:T(8,128)S(1)}, u32[]{:S(2)}, u32[]{:S(2)}) %collective-permute-start.22) | collective-permute-done | bytes 139296 | tf_op jit(solution)/shard_map/ppermute | solution.py:25
  438.7 3.9 copy.14
  (313 shorter events, 20.0 us)
Async XLA Ops:
  7.2 149.9 %all-gather.2.cloned.1.call-start = ((), (), s32[]{:S(2)}) async-start(), calls=%async_computation.3 | async-start | bytes 3145728 | tf_op jit(solution)/shard_map/all_gather | solution.py:100
  8.0 8.0 %collective-permute-start = (bf16[1,1,2048]{2,1,0:T(2,128)(2,1)S(1)}, bf16[1,1,2048]{2,1,0:T(2,128)(2,1)S(1)}, u32[]{:S(2)}, u32[]{:S(2)}) collective-permute-start(bf16[1,1,2048]{2,1,0:T(2,128)(2,1)S(1)} %slice.106), channel_id=1, source_target_pairs={{0,4},{4,8},{8,12},{1,5},{5,9},{9,13},{2,6},{6,10},{10,14},{3,7},{... | collective-permute-start | bytes 12296 | tf_op jit(solution)/shard_map/ppermute | solution.py:13
  15.9 26.8 %copy-start.112 = (pred[256]{0:T(512)(128)(4,1)}, pred[256]{0:T(512)(128)(4,1)S(1)}, u32[]{:S(2)}) copy-start(pred[256]{0:T(512)(128)(4,1)S(1)} %get-tuple-element.149) | copy-start | bytes 772
  15.9 35.3 %copy-start.99 = (pred[256]{0:T(512)(128)(4,1)}, pred[256]{0:T(512)(128)(4,1)S(1)}, u32[]{:S(2)}) copy-start(pred[256]{0:T(512)(128)(4,1)S(1)} %get-tuple-element.148) | copy-start | bytes 772
  16.0 46.5 %copy-start.104 = (pred[256]{0:T(512)(128)(4,1)}, pred[256]{0:T(512)(128)(4,1)S(1)}, u32[]{:S(2)}) copy-start(pred[256]{0:T(512)(128)(4,1)S(1)} %get-tuple-element.147) | copy-start | bytes 772
  16.0 60.5 %copy-start.101 = (pred[256]{0:T(512)(128)(4,1)}, pred[256]{0:T(512)(128)(4,1)S(1)}, u32[]{:S(2)}) copy-start(pred[256]{0:T(512)(128)(4,1)S(1)} %get-tuple-element.146) | copy-start | bytes 772
  18.3 111.7 %copy-start = (bf16[1,256,2048]{2,1,0:T(8,128)(2,1)}, bf16[1,256,2048]{2,1,0:T(8,128)(2,1)S(1)}, u32[]{:S(2)}) copy-start(bf16[1,256,2048]{2,1,0:T(8,128)(2,1)S(1)} %fusion.18) | copy-start | bytes 3145732
  18.3 4.8 %collective-permute-start.1 = (bf16[1,2,2048]{2,1,0:T(2,128)(2,1)S(1)}, bf16[1,2,2048]{2,1,0:T(2,128)(2,1)S(1)}, u32[]{:S(2)}, u32[]{:S(2)}) collective-permute-start(bf16[1,2,2048]{2,1,0:T(2,128)(2,1)S(1)} %slice.156), channel_id=1, source_target_pairs={{0,4},{4,8},{8,12},{1,5},{5,9},{9,13},{2,6},{6,10},{10,14},{3,7},{... | collective-permute-start | bytes 24584 | tf_op jit(solution)/shard_map/ppermute | solution.py:13
  23.9 5.6 %collective-permute-start.2 = (bf16[1,4,2048]{2,1,0:T(4,128)(2,1)S(1)}, bf16[1,4,2048]{2,1,0:T(4,128)(2,1)S(1)}, u32[]{:S(2)}, u32[]{:S(2)}) collective-permute-start(bf16[1,4,2048]{2,1,0:T(4,128)(2,1)S(1)} %slice.158), channel_id=1, source_target_pairs={{0,4},{4,8},{8,12},{1,5},{5,9},{9,13},{2,6},{6,10},{10,14},{3,7},{... | collective-permute-start | bytes 49160 | tf_op jit(solution)/shard_map/ppermute | solution.py:13
  30.3 5.8 %collective-permute-start.3 = (bf16[1,8,2048]{2,1,0:T(8,128)(2,1)S(1)}, bf16[1,8,2048]{2,1,0:T(8,128)(2,1)S(1)}, u32[]{:S(2)}, u32[]{:S(2)}) collective-permute-start(bf16[1,8,2048]{2,1,0:T(8,128)(2,1)S(1)} %slice.160), channel_id=1, source_target_pairs={{0,4},{4,8},{8,12},{1,5},{5,9},{9,13},{2,6},{6,10},{10,14},{3,7},{... | collective-permute-start | bytes 98312 | tf_op jit(solution)/shard_map/ppermute | solution.py:13
  36.6 6.1 %collective-permute-start.4 = (bf16[1,16,2048]{2,1,0:T(8,128)(2,1)S(1)}, bf16[1,16,2048]{2,1,0:T(8,128)(2,1)S(1)}, u32[]{:S(2)}, u32[]{:S(2)}) collective-permute-start(bf16[1,16,2048]{2,1,0:T(8,128)(2,1)S(1)} %slice.162), channel_id=1, source_target_pairs={{0,4},{4,8},{8,12},{1,5},{5,9},{9,13},{2,6},{6,10},{10,14},{3,7},{... | collective-permute-start | bytes 196616 | tf_op jit(solution)/shard_map/ppermute | solution.py:13
  43.4 7.9 %collective-permute-start.5 = (bf16[1,32,2048]{2,1,0:T(8,128)(2,1)S(1)}, bf16[1,32,2048]{2,1,0:T(8,128)(2,1)S(1)}, u32[]{:S(2)}, u32[]{:S(2)}) collective-permute-start(bf16[1,32,2048]{2,1,0:T(8,128)(2,1)S(1)} %slice.164), channel_id=1, source_target_pairs={{0,4},{4,8},{8,12},{1,5},{5,9},{9,13},{2,6},{6,10},{10,14},{3,7},{... | collective-permute-start | bytes 393224 | tf_op jit(solution)/shard_map/ppermute | solution.py:13
  51.9 10.6 %collective-permute-start.6 = (bf16[1,64,2048]{2,1,0:T(8,128)(2,1)S(1)}, bf16[1,64,2048]{2,1,0:T(8,128)(2,1)S(1)}, u32[]{:S(2)}, u32[]{:S(2)}) collective-permute-start(bf16[1,64,2048]{2,1,0:T(8,128)(2,1)S(1)} %slice.166), channel_id=1, source_target_pairs={{0,4},{4,8},{8,12},{1,5},{5,9},{9,13},{2,6},{6,10},{10,14},{3,7},{... | collective-permute-start | bytes 786440 | tf_op jit(solution)/shard_map/ppermute | solution.py:13
  63.2 13.3 %collective-permute-start.7 = (bf16[1,128,2048]{2,1,0:T(8,128)(2,1)S(1)}, bf16[1,128,2048]{2,1,0:T(8,128)(2,1)S(1)}, u32[]{:S(2)}, u32[]{:S(2)}) collective-permute-start(bf16[1,128,2048]{2,1,0:T(8,128)(2,1)S(1)} %get-tuple-element.123), channel_id=1, source_target_pairs={{0,4},{4,8},{8,12},{1,5},{5,9},{9,13},{2,6},{6,10},{10,14},{3,7},{... | collective-permute-start | bytes 1572872 | tf_op jit(solution)/shard_map/ppermute | solution.py:13
  78.0 52.0 %copy-start.2 = (bf16[1,256,2048]{2,1,0:T(8,128)(2,1)S(1)}, bf16[1,256,2048]{2,1,0:T(8,128)(2,1)}, u32[]{:S(2)}) copy-start(bf16[1,256,2048]{2,1,0:T(8,128)(2,1)} %param.7) | copy-start | bytes 3145732
  78.0 20.4 %collective-permute-start.8 = (bf16[1,256,2048]{2,1,0:T(8,128)(2,1)}, bf16[1,256,2048]{2,1,0:T(8,128)(2,1)}, u32[]{:S(2)}, u32[]{:S(2)}) collective-permute-start(bf16[1,256,2048]{2,1,0:T(8,128)(2,1)} %fusion.52), channel_id=1, source_target_pairs={{0,4},{4,8},{8,12},{1,5},{5,9},{9,13},{2,6},{6,10},{10,14},{3,7},{... | collective-permute-start | bytes 3145736 | tf_op jit(solution)/shard_map/ppermute | solution.py:13
  83.6 321.8 %reduce-scatter.3.cloned.1.call-start = ((), (), s32[]{:S(2)}) async-start(), calls=%async_computation.2 | async-start | bytes 3145728 | tf_op jit(solution)/shard_map/reduce_scatter | solution.py:96
  83.6 46.4 %copy-start.5 = (bf16[1,256,2048]{2,1,0:T(8,128)(2,1)S(1)}, bf16[1,256,2048]{2,1,0:T(8,128)(2,1)}, u32[]{:S(2)}) copy-start(bf16[1,256,2048]{2,1,0:T(8,128)(2,1)} %copy-done.4) | copy-start | bytes 3145732
  83.6 46.4 %copy-start.8 = (bf16[1,256,2048]{2,1,0:T(8,128)(2,1)S(1)}, bf16[1,256,2048]{2,1,0:T(8,128)(2,1)}, u32[]{:S(2)}) copy-start(bf16[1,256,2048]{2,1,0:T(8,128)(2,1)} %copy-done.7) | copy-start | bytes 3145732
  83.6 46.4 %copy-start.11 = (bf16[1,256,2048]{2,1,0:T(8,128)(2,1)S(1)}, bf16[1,256,2048]{2,1,0:T(8,128)(2,1)}, u32[]{:S(2)}) copy-start(bf16[1,256,2048]{2,1,0:T(8,128)(2,1)} %copy-done.10) | copy-start | bytes 3145732
  83.7 46.4 %copy-start.102 = (pred[256]{0:T(512)(128)(4,1)S(1)}, pred[256]{0:T(512)(128)(4,1)}, u32[]{:S(2)}) copy-start(pred[256]{0:T(512)(128)(4,1)} %copy-done.101) | copy-start | bytes 772
  100.4 43.7 %copy-start.28 = (bf16[1,256,2048]{2,1,0:T(8,128)(2,1)}, bf16[1,256,2048]{2,1,0:T(8,128)(2,1)S(1)}, u32[]{:S(2)}) copy-start(bf16[1,256,2048]{2,1,0:T(8,128)(2,1)S(1)} %fusion.57) | copy-start | bytes 3145732
  100.4 29.5 %collective-permute-start.9 = (bf16[1,256,2048]{2,1,0:T(8,128)(2,1)S(1)}, bf16[1,256,2048]{2,1,0:T(8,128)(2,1)S(1)}, u32[]{:S(2)}, u32[]{:S(2)}) collective-permute-start(bf16[1,256,2048]{2,1,0:T(8,128)(2,1)S(1)} %fusion.57), channel_id=1, source_target_pairs={{0,8},{4,12},{1,9},{5,13},{2,10},{6,14},{3,11},{7,15},{16,24},{20,... | collective-permute-start | bytes 3145736 | tf_op jit(solution)/shard_map/ppermute | solution.py:13
  119.0 25.2 %copy-start.71 = (f32[2048]{0:T(1024)}, f32[2048]{0:T(1024)S(1)}, u32[]{:S(2)}) copy-start(f32[2048]{0:T(1024)S(1)} %get-tuple-element.154) | copy-start | bytes 24580
  119.0 25.2 %copy-start.73 = (f32[2048]{0:T(1024)}, f32[2048]{0:T(1024)S(1)}, u32[]{:S(2)}) copy-start(f32[2048]{0:T(1024)S(1)} %get-tuple-element.155) | copy-start | bytes 24580
  120.7 23.5 %copy-start.41 = (f32[1,2048]{1,0:T(1,128)}, f32[1,2048]{1,0:T(1,128)S(1)}, u32[]{:S(2)}) copy-start(f32[1,2048]{1,0:T(1,128)S(1)} %get-tuple-element.137) | copy-start | bytes 24580
  120.7 23.5 %copy-start.43 = (f32[1,2048]{1,0:T(1,128)}, f32[1,2048]{1,0:T(1,128)S(1)}, u32[]{:S(2)}) copy-start(f32[1,2048]{1,0:T(1,128)S(1)} %get-tuple-element.133) | copy-start | bytes 24580
  120.7 23.5 %copy-start.45 = (f32[1,2048]{1,0:T(1,128)}, f32[1,2048]{1,0:T(1,128)S(1)}, u32[]{:S(2)}) copy-start(f32[1,2048]{1,0:T(1,128)S(1)} %get-tuple-element.131) | copy-start | bytes 24580
  120.7 23.5 %copy-start.47 = (f32[1,2048]{1,0:T(1,128)}, f32[1,2048]{1,0:T(1,128)S(1)}, u32[]{:S(2)}) copy-start(f32[1,2048]{1,0:T(1,128)S(1)} %get-tuple-element.132) | copy-start | bytes 24580
  120.7 23.5 %copy-start.49 = (f32[1,2048]{1,0:T(1,128)}, f32[1,2048]{1,0:T(1,128)S(1)}, u32[]{:S(2)}) copy-start(f32[1,2048]{1,0:T(1,128)S(1)} %get-tuple-element.130) | copy-start | bytes 24580
  120.7 23.5 %copy-start.55 = (f32[1,2048]{1,0:T(1,128)}, f32[1,2048]{1,0:T(1,128)S(1)}, u32[]{:S(2)}) copy-start(f32[1,2048]{1,0:T(1,128)S(1)} %get-tuple-element.127) | copy-start | bytes 24580
  120.7 23.5 %copy-start.57 = (f32[1,2048]{1,0:T(1,128)}, f32[1,2048]{1,0:T(1,128)S(1)}, u32[]{:S(2)}) copy-start(f32[1,2048]{1,0:T(1,128)S(1)} %get-tuple-element.136) | copy-start | bytes 24580
  156.8 281.9 %reduce-scatter.5.cloned.1.call-start = ((), (), s32[]{:S(2)}) async-start(), calls=%async_computation.4 | async-start | bytes 18874368 | tf_op jit(solution)/shard_map/reduce_scatter | solution.py:107
  179.6 63.5 %copy-start.29 = (bf16[1,256,2048]{2,1,0:T(8,128)(2,1)S(1)}, bf16[1,256,2048]{2,1,0:T(8,128)(2,1)}, u32[]{:S(2)}) copy-start(bf16[1,256,2048]{2,1,0:T(8,128)(2,1)} %copy-done.28) | copy-start | bytes 3145732
  179.6 63.5 %copy-start.36 = (bf16[1,256,2048]{2,1,0:T(8,128)(2,1)S(1)}, bf16[1,256,2048]{2,1,0:T(8,128)(2,1)}, u32[]{:S(2)}) copy-start(bf16[1,256,2048]{2,1,0:T(8,128)(2,1)} %copy-done.35) | copy-start | bytes 3145732
  179.6 63.5 %copy-start.37 = (bf16[1,256,2048]{2,1,0:T(8,128)(2,1)S(1)}, bf16[1,256,2048]{2,1,0:T(8,128)(2,1)}, u32[]{:S(2)}) copy-start(bf16[1,256,2048]{2,1,0:T(8,128)(2,1)} %get-tuple-element.115) | copy-start | bytes 3145732
  179.6 63.5 %copy-start.50 = (f32[1,2048]{1,0:T(1,128)S(1)}, f32[1,2048]{1,0:T(1,128)}, u32[]{:S(2)}) copy-start(f32[1,2048]{1,0:T(1,128)} %copy-done.49) | copy-start | bytes 24580
  179.7 63.5 %copy-start.64 = (f32[1,2048]{1,0:T(1,128)S(1)}, f32[1,2048]{1,0:T(1,128)}, u32[]{:S(2)}) copy-start(f32[1,2048]{1,0:T(1,128)} %copy-done.63) | copy-start | bytes 24580
  179.7 63.5 %copy-start.66 = (f32[1,2048]{1,0:T(1,128)S(1)}, f32[1,2048]{1,0:T(1,128)}, u32[]{:S(2)}) copy-start(f32[1,2048]{1,0:T(1,128)} %copy-done.65) | copy-start | bytes 24580
  179.7 63.5 %copy-start.68 = (f32[1,2048]{1,0:T(1,128)S(1)}, f32[1,2048]{1,0:T(1,128)}, u32[]{:S(2)}) copy-start(f32[1,2048]{1,0:T(1,128)} %copy-done.67) | copy-start | bytes 24580
  179.7 63.5 %copy-start.70 = (f32[1,2048]{1,0:T(1,128)S(1)}, f32[1,2048]{1,0:T(1,128)}, u32[]{:S(2)}) copy-start(f32[1,2048]{1,0:T(1,128)} %copy-done.69) | copy-start | bytes 24580
  179.7 63.5 %copy-start.72 = (f32[2048]{0:T(1024)S(1)}, f32[2048]{0:T(1024)}, u32[]{:S(2)}) copy-start(f32[2048]{0:T(1024)} %copy-done.71) | copy-start | bytes 24580
  179.7 63.5 %copy-start.74 = (f32[2048]{0:T(1024)S(1)}, f32[2048]{0:T(1024)}, u32[]{:S(2)}) copy-start(f32[2048]{0:T(1024)} %copy-done.73) | copy-start | bytes 24580
  179.7 63.5 %copy-start.115 = (pred[256]{0:T(512)(128)(4,1)S(1)}, pred[256]{0:T(512)(128)(4,1)}, u32[]{:S(2)}) copy-start(pred[256]{0:T(512)(128)(4,1)} %get-tuple-element.145) | copy-start | bytes 772
  179.7 63.5 %copy-start.118 = (pred[256]{0:T(512)(128)(4,1)S(1)}, pred[256]{0:T(512)(128)(4,1)}, u32[]{:S(2)}) copy-start(pred[256]{0:T(512)(128)(4,1)} %get-tuple-element.144) | copy-start | bytes 772
  183.9 59.2 %collective-permute-start.10 = (bf16[1,256,2048]{2,1,0:T(8,128)(2,1)S(1)}, bf16[1,256,2048]{2,1,0:T(8,128)(2,1)S(1)}, u32[]{:S(2)}, u32[]{:S(2)}) collective-permute-start(bf16[1,256,2048]{2,1,0:T(8,128)(2,1)S(1)} %get-tuple-element.112), channel_id=1, source_target_pairs={{8,0},{12,4},{9,1},{13,5},{10,2},{14,6},{11,3},{15,7},{24,16},{28,... | collective-permute-start | bytes 3145736 | tf_op jit(solution)/shard_map/ppermute | solution.py:13
  251.7 49.6 %copy-start.27 = (bf16[1,128,2048]{2,1,0:T(8,128)(2,1)S(1)}, bf16[1,128,2048]{2,1,0:T(8,128)(2,1)}, u32[]{:S(2)}) copy-start(bf16[1,128,2048]{2,1,0:T(8,128)(2,1)} %copy-done.26) | copy-start | bytes 1572868
  251.7 49.6 %copy-start.32 = (bf16[1,128,2048]{2,1,0:T(8,128)(2,1)S(1)}, bf16[1,128,2048]{2,1,0:T(8,128)(2,1)}, u32[]{:S(2)}) copy-start(bf16[1,128,2048]{2,1,0:T(8,128)(2,1)} %copy-done.31) | copy-start | bytes 1572868
  251.7 49.6 %copy-start.103 = (pred[256]{0:T(512)(128)(4,1)S(1)}, pred[256]{0:T(512)(128)(4,1)}, u32[]{:S(2)}) copy-start(pred[256]{0:T(512)(128)(4,1)} %copy-done.101) | copy-start | bytes 772
  252.2 50.1 %copy-start.46 = (f32[1,2048]{1,0:T(1,128)S(1)}, f32[1,2048]{1,0:T(1,128)}, u32[]{:S(2)}) copy-start(f32[1,2048]{1,0:T(1,128)} %copy-done.45) | copy-start | bytes 24580
  252.2 49.1 %collective-permute-start.11 = (bf16[1,256,2048]{2,1,0:T(8,128)(2,1)S(1)}, bf16[1,256,2048]{2,1,0:T(8,128)(2,1)S(1)}, u32[]{:S(2)}, u32[]{:S(2)}) collective-permute-start(bf16[1,256,2048]{2,1,0:T(8,128)(2,1)S(1)} %fusion.96), channel_id=1, source_target_pairs={{4,0},{8,4},{12,8},{5,1},{9,5},{13,9},{6,2},{10,6},{14,10},{7,3},{... | collective-permute-start | bytes 3145736 | tf_op jit(solution)/shard_map/ppermute | solution.py:13
  302.7 26.0 %copy-start.24 = (bf16[1,192,2048]{2,1,0:T(8,128)(2,1)S(1)}, bf16[1,192,2048]{2,1,0:T(8,128)(2,1)}, u32[]{:S(2)}) copy-start(bf16[1,192,2048]{2,1,0:T(8,128)(2,1)} %copy-done.23) | copy-start | bytes 2359300
  302.8 26.0 %copy-start.105 = (pred[256]{0:T(512)(128)(4,1)S(1)}, pred[256]{0:T(512)(128)(4,1)}, u32[]{:S(2)}) copy-start(pred[256]{0:T(512)(128)(4,1)} %copy-done.104) | copy-start | bytes 772
  302.9 25.9 %collective-permute-start.12 = (bf16[1,128,2048]{2,1,0:T(8,128)(2,1)S(1)}, bf16[1,128,2048]{2,1,0:T(8,128)(2,1)S(1)}, u32[]{:S(2)}, u32[]{:S(2)}) collective-permute-start(bf16[1,128,2048]{2,1,0:T(8,128)(2,1)S(1)} %get-tuple-element.122), channel_id=1, source_target_pairs={{4,0},{8,4},{12,8},{5,1},{9,5},{13,9},{6,2},{10,6},{14,10},{7,3},{... | collective-permute-start | bytes 1572872 | tf_op jit(solution)/shard_map/ppermute | solution.py:13
  330.3 15.6 %collective-permute-start.13 = (bf16[1,64,2048]{2,1,0:T(8,128)(2,1)S(1)}, bf16[1,64,2048]{2,1,0:T(8,128)(2,1)S(1)}, u32[]{:S(2)}, u32[]{:S(2)}) collective-permute-start(bf16[1,64,2048]{2,1,0:T(8,128)(2,1)S(1)} %slice.173), channel_id=1, source_target_pairs={{4,0},{8,4},{12,8},{5,1},{9,5},{13,9},{6,2},{10,6},{14,10},{7,3},{... | collective-permute-start | bytes 786440 | tf_op jit(solution)/shard_map/ppermute | solution.py:13
  347.4 10.7 %collective-permute-start.14 = (bf16[1,32,2048]{2,1,0:T(8,128)(2,1)S(1)}, bf16[1,32,2048]{2,1,0:T(8,128)(2,1)S(1)}, u32[]{:S(2)}, u32[]{:S(2)}) collective-permute-start(bf16[1,32,2048]{2,1,0:T(8,128)(2,1)S(1)} %slice.175), channel_id=1, source_target_pairs={{4,0},{8,4},{12,8},{5,1},{9,5},{13,9},{6,2},{10,6},{14,10},{7,3},{... | collective-permute-start | bytes 393224 | tf_op jit(solution)/shard_map/ppermute | solution.py:13
  362.9 8.7 %collective-permute-start.15 = (bf16[1,16,2048]{2,1,0:T(8,128)(2,1)S(1)}, bf16[1,16,2048]{2,1,0:T(8,128)(2,1)S(1)}, u32[]{:S(2)}, u32[]{:S(2)}) collective-permute-start(bf16[1,16,2048]{2,1,0:T(8,128)(2,1)S(1)} %slice.354), channel_id=1, source_target_pairs={{4,0},{8,4},{12,8},{5,1},{9,5},{13,9},{6,2},{10,6},{14,10},{7,3},{... | collective-permute-start | bytes 196616 | tf_op jit(solution)/shard_map/ppermute | solution.py:13
  376.8 7.0 %collective-permute-start.16 = (bf16[1,8,2048]{2,1,0:T(8,128)(2,1)S(1)}, bf16[1,8,2048]{2,1,0:T(8,128)(2,1)S(1)}, u32[]{:S(2)}, u32[]{:S(2)}) collective-permute-start(bf16[1,8,2048]{2,1,0:T(8,128)(2,1)S(1)} %slice.356), channel_id=1, source_target_pairs={{4,0},{8,4},{12,8},{5,1},{9,5},{13,9},{6,2},{10,6},{14,10},{7,3},{... | collective-permute-start | bytes 98312 | tf_op jit(solution)/shard_map/ppermute | solution.py:13
  389.1 6.5 %collective-permute-start.17 = (bf16[1,4,2048]{2,1,0:T(4,128)(2,1)S(1)}, bf16[1,4,2048]{2,1,0:T(4,128)(2,1)S(1)}, u32[]{:S(2)}, u32[]{:S(2)}) collective-permute-start(bf16[1,4,2048]{2,1,0:T(4,128)(2,1)S(1)} %slice.358), channel_id=1, source_target_pairs={{4,0},{8,4},{12,8},{5,1},{9,5},{13,9},{6,2},{10,6},{14,10},{7,3},{... | collective-permute-start | bytes 49160 | tf_op jit(solution)/shard_map/ppermute | solution.py:13
  397.2 6.1 %collective-permute-start.18 = (bf16[1,2,2048]{2,1,0:T(2,128)(2,1)S(1)}, bf16[1,2,2048]{2,1,0:T(2,128)(2,1)S(1)}, u32[]{:S(2)}, u32[]{:S(2)}) collective-permute-start(bf16[1,2,2048]{2,1,0:T(2,128)(2,1)S(1)} %slice.360), channel_id=1, source_target_pairs={{4,0},{8,4},{12,8},{5,1},{9,5},{13,9},{6,2},{10,6},{14,10},{7,3},{... | collective-permute-start | bytes 24584 | tf_op jit(solution)/shard_map/ppermute | solution.py:13
  417.5 1.5 collective-permute-start.20
  419.1 7.1 %collective-permute-start.21 = (f32[17,2048]{1,0:T(8,128)S(1)}, f32[17,2048]{1,0:T(8,128)S(1)}, u32[]{:S(2)}, u32[]{:S(2)}) collective-permute-start(f32[17,2048]{1,0:T(8,128)S(1)} %fusion.169), channel_id=1, source_target_pairs={{0,4},{4,0},{8,12},{12,8},{1,5},{5,1},{9,13},{13,9},{2,6},{6,2},{1... | collective-permute-start | bytes 417800 | tf_op jit(solution)/shard_map/ppermute | solution.py:25
  419.9 6.4 %collective-permute-start.19 = (bf16[1,1,2048]{2,1,0:T(2,128)(2,1)S(1)}, bf16[1,1,2048]{2,1,0:T(2,128)(2,1)S(1)}, u32[]{:S(2)}, u32[]{:S(2)}) collective-permute-start(bf16[1,1,2048]{2,1,0:T(2,128)(2,1)S(1)} %slice.362), channel_id=1, source_target_pairs={{4,0},{8,4},{12,8},{5,1},{9,5},{13,9},{6,2},{10,6},{14,10},{7,3},{... | collective-permute-start | bytes 12296 | tf_op jit(solution)/shard_map/ppermute | solution.py:13
  426.2 11.2 %collective-permute-start.22 = (f32[17,2048]{1,0:T(8,128)S(1)}, f32[17,2048]{1,0:T(8,128)S(1)}, u32[]{:S(2)}, u32[]{:S(2)}) collective-permute-start(f32[17,2048]{1,0:T(8,128)S(1)} %add.972), channel_id=1, source_target_pairs={{0,8},{4,12},{8,0},{12,4},{1,9},{5,13},{9,1},{13,5},{2,10},{6,14},... | collective-permute-start | bytes 417800 | tf_op jit(solution)/shard_map/ppermute | solution.py:25
  (81 other events, 852.1 us)
Sparse Core Ops, SparseCore 0:
  83.7 32.1 all-gather.1
  156.9 45.5 reduce-scatter.2
  205.0 216.6 reduce-scatter.4

commit v2 on v1

--- a/solution.py
+++ b/solution.py
@@ -59,6 +59,8 @@
     positions = offset + jnp.arange(row_count, dtype=jnp.int32)
     starts = doc_starts(positions, doc_lengths)
     shallow = min(levels, row_count.bit_length() - 1)
+    gathered = lax.all_gather(out_grad, "tensor", axis=2, tiled=True)
+    grad_rows = lax.all_to_all(gathered, ("seq", "dp"), 2, 1, tiled=True)
     summed = jnp.zeros(tokens.shape, jnp.float32)
     states = [tokens]
     previous_list = []
@@ -75,6 +77,8 @@
         previous_list.append(previous)
         states.append(current)
     for level_index in range(shallow, levels):
+        if level_index == shallow:
+            grad_rows, current = lax.optimization_barrier((grad_rows, current))
         spacing = 2**level_index
         device_hops = spacing // row_count
         if device_hops < seq_count:
@@ -97,19 +101,12 @@
         partial_mix.astype(jnp.bfloat16), "tensor", scatter_dimension=2, tiled=True
     ).astype(jnp.float32)
     result = (tokens.astype(jnp.float32) + mixed).astype(jnp.bfloat16)
-    gathered = lax.all_gather(out_grad, "tensor", axis=2, tiled=True)
     act_grad = jnp.einsum("bro,oc->brc", gathered, mix_weight, preferred_element_type=jnp.float32)
-    weight_part = (
-        jnp.einsum("bro,brc->oc", gathered, activated, preferred_element_type=jnp.float32)
+    act_all = lax.all_gather(activated, ("seq", "dp"), axis=1, tiled=True)
+    weight_grad = (
+        jnp.einsum("bto,bti->oi", grad_rows, act_all, preferred_element_type=jnp.float32)
         * grad_scale
     ).astype(jnp.bfloat16)
-    weight_part, act_grad = lax.optimization_barrier((weight_part, act_grad))
-    weight_grad = lax.psum_scatter(
-        weight_part,
-        ("seq", "dp"),
-        scatter_dimension=0,
-        tiled=True,
-    )
     summed_grad = act_grad * gelu_slope(summed)
     carry_grad = (level_weights[levels] * summed_grad).astype(jnp.bfloat16)
     weight_sums = [None] * (levels + 1)
@@ -119,6 +116,8 @@
     high_first = jnp.zeros((channels,), jnp.float32)
     high_second = jnp.zeros((channels,), jnp.float32)
     for level_index in range(levels - 1, -1, -1):
+        if level_index == min(3, levels - 1):
+            weight_grad, carry_grad = lax.optimization_barrier((weight_grad, carry_grad))
         spacing = 2**level_index
         current = states[level_index]
         previous = previous_list[level_index]

time: 457 us -> 553 us (1.21)
  local copies, waits for them, and re-layouts: 14.2 us -> 44.4 us
  waiting for transfers between devices: 239 us -> 263 us
  other arithmetic: 73.5 us -> 95.3 us
  starting transfers between devices: 72 us -> 90.6 us
    unnamed x0 -> x1, other arithmetic: none -> 22.9 us
    ppermute x20, waiting for transfers between devices: 223 us -> 240 us  [shifted_2(): return lax.ppermute(block, axis, route)]
    convert_element_type x0 -> x2, other arithmetic: none -> 15.6 us  [the longest x1 14 us: shards(): activated = gelu_value(summed).astype(jnp.bfloat16)]
    unnamed x239 -> x326, local copies, waits for them, and re-layouts: 4.52 us -> 19.5 us
    add x1 -> x0, other arithmetic: 14.1 us -> none  [shards(): summed = summed + level_weights[levels] * current]
    all_gather x1, waiting for transfers between devices: 0.02 us -> 10.9 us  [shards(): gathered = lax.all_gather(out_grad, 'tensor', axis=2, tiled=True)]
    all_gather x0 -> x1, local copies, waits for them, and re-layouts: none -> 10 us  [shards(): gathered = lax.all_gather(out_grad, 'tensor', axis=2, tiled=True)]
    ppermute x20, starting transfers between devices: 71.5 us -> 81.1 us  [shifted_2(): return lax.ppermute(block, axis, route)]
  transfers between devices with their start and end apart: 26 -> 27, of which waited for: 21 -> 20; matrix products, arithmetic and copies ran while one was open for 24% -> 23% of each run, Pallas kernels for 0% -> 0%
where the time goes in v2:
time: 553 us; the launch traced here: 543 us
  waiting for transfers between devices  263 us (48%)
  other arithmetic  95.3 us (17%)
  starting transfers between devices  90.6 us (16%)
  local copies, waits for them, and re-layouts  44.4 us (8%)
  matrix products  33.1 us (6%)
  between operations  16.6 us (3%)
    ppermute x20, waiting for transfers between devices, shifted_2(): return lax.ppermute(block, axis, route)  240 us
    ppermute x20, starting transfers between devices, shifted_2(): return lax.ppermute(block, axis, route)  81.1 us
    unnamed x1, other arithmetic  22.9 us
    unnamed x326, local copies, waits for them, and re-layouts  19.5 us
    reduce_sum x4, other arithmetic, shards(): jnp.sum(weighted * previous.astype(jnp.float32), axis=(0, 1))  19.2 us
    convert_element_type x1, other arithmetic, shards(): activated = gelu_value(summed).astype(jnp.bfloat16)  14 us
    dot_general x1, matrix products, shards(): jnp.einsum('brc,oc->bro', activated, mix_weight, preferred_element_type=j...  12 us
    ppermute x3, waiting for transfers between devices, exchange_sum(): values = values + lax.ppermute(values, axis, route)  11.5 us
  transfers between devices with their start and end apart: 27, of which 20 were waited for; matrix products, arithmetic and copies ran while one was open for 23% of the time, Pallas kernels for 0%

profile of v2, /device:TPU:0, one launch (start us, length us, event | category | flops | bytes accessed | tf_op | source)
XLA Modules:
  0.0 542.6 jit_solution(16825817181484727236)
XLA Ops:
  8.0 4.9 collective-permute-start
  16.0 2.3 fusion.33
  18.3 3.5 collective-permute-start.1
  23.9 4.2 collective-permute-start.2
  28.1 1.4 collective-permute-done.2
  30.3 4.2 collective-permute-start.3
  35.6 10.9 %all-gather.3.cloned.1.call-done = bf16[1,256,4096]{2,1,0:T(8,128)(2,1)} async-done(((bf16[1,256,2048]{2,1,0:T(8,128)(2,1)}), bf16[1,256,4096]{2,1,0:T(8,128)(2,1)}) %all-gather.3.cloned.1.call-update) | async-done | bytes 2097168 | tf_op jit(solution)/shard_map/all_gather | solution.py:62
  46.5 10.0 %copy.19 = bf16[1,256,4096]{1,0,2:T(2,128)(2,1)} copy(bf16[1,256,4096]{2,1,0:T(8,128)(2,1)} %all-gather.3.cloned.1.call-done) | data formatting | bytes 4194304 | tf_op jit(solution)/shard_map/all_gather | solution.py:62
  57.0 22.9 %reduce.1 = bf16[4096,256]{1,0:T(8,128)(2,1)} reduce(bf16[4096,1,256]{2,1,0:T(2,128)(2,1)} %bitcast.81, bf16[]{:T(256)} %broadcast.1212), dimensions={1}, to_apply=%bitcast.60.reduce_sub_computation | reduce | bytes 4194306
  79.9 5.8 %reshape.2423 = bf16[8,2,65536]{2,1,0:T(2,128)(2,1)} reshape(bf16[4096,256]{1,0:T(8,128)(2,1)} %reduce.1) | data formatting | bytes 4194304
  85.7 4.6 all-to-all-start
  90.4 1.7 fusion.47
  92.1 3.9 collective-permute-start.4
  96.1 30.4 %collective-permute-done.4 = bf16[1,16,2048]{2,1,0:T(8,128)(2,1)S(1)} collective-permute-done((bf16[1,16,2048]{2,1,0:T(8,128)(2,1)S(1)}, bf16[1,16,2048]{2,1,0:T(8,128)(2,1)S(1)}, u32[]{:S(2)}, u32[]{:S(2)}) %collective-permute-start.4) | collective-permute-done | bytes 65568 | tf_op jit(solution)/shard_map/ppermute | solution.py:13
  127.2 14.6 %collective-permute-start.5 = (bf16[1,32,2048]{2,1,0:T(8,128)(2,1)S(1)}, bf16[1,32,2048]{2,1,0:T(8,128)(2,1)S(1)}, u32[]{:S(2)}, u32[]{:S(2)}) collective-permute-start(bf16[1,32,2048]{2,1,0:T(8,128)(2,1)S(1)} %slice.164), channel_id=1, source_target_pairs={{0,4},{4,8},{8,12},{1,5},{5,9},{9,13},{2,6},{6,10},{10,14},{3,7},{... | collective-permute-start | bytes 393224 | tf_op jit(solution)/shard_map/ppermute | solution.py:13
  141.8 2.9 collective-permute-done.5
  145.3 4.4 collective-permute-start.6
  149.8 4.8 collective-permute-done.6
  155.3 4.4 collective-permute-start.7
  159.7 9.6 %collective-permute-done.7 = bf16[1,128,2048]{2,1,0:T(8,128)(2,1)S(1)} collective-permute-done((bf16[1,128,2048]{2,1,0:T(8,128)(2,1)S(1)}, bf16[1,128,2048]{2,1,0:T(8,128)(2,1)S(1)}, u32[]{:S(2)}, u32[]{:S(2)}) %collective-permute-start.7) | collective-permute-done | bytes 524320 | tf_op jit(solution)/shard_map/ppermute | solution.py:13
  170.1 1.5 fusion.67
  171.7 6.8 %reshape.2424 = bf16[4096,1,256]{2,1,0:T(2,128)(2,1)} reshape(bf16[8,2,65536]{2,1,0:T(2,128)(2,1)} %all-to-all-done) | data formatting | bytes 4194304
  178.4 3.9 copy.21
  182.3 4.0 copy.20
  186.4 4.7 collective-permute-start.8
  191.1 20.2 %collective-permute-done.8 = bf16[1,256,2048]{2,1,0:T(8,128)(2,1)S(1)} collective-permute-done((bf16[1,256,2048]{2,1,0:T(8,128)(2,1)}, bf16[1,256,2048]{2,1,0:T(8,128)(2,1)S(1)}, u32[]{:S(2)}, u32[]{:S(2)}) %collective-permute-start.8) | collective-permute-done | bytes 1048608 | tf_op jit(solution)/shard_map/ppermute | solution.py:13
  211.3 2.1 fusion.17
  213.5 6.5 %collective-permute-start.9 = (bf16[1,256,2048]{2,1,0:T(8,128)(2,1)S(1)}, bf16[1,256,2048]{2,1,0:T(8,128)(2,1)S(1)}, u32[]{:S(2)}, u32[]{:S(2)}) collective-permute-start(bf16[1,256,2048]{2,1,0:T(8,128)(2,1)S(1)} %fusion.17), channel_id=1, source_target_pairs={{0,8},{4,12},{1,9},{5,13},{2,10},{6,14},{3,11},{7,15},{16,24},{20,... | collective-permute-start | bytes 3145736 | tf_op jit(solution)/shard_map/ppermute | solution.py:13
  220.9 1.7 fusion.191
  222.7 16.1 %collective-permute-done.9 = bf16[1,256,2048]{2,1,0:T(8,128)(2,1)S(1)} collective-permute-done((bf16[1,256,2048]{2,1,0:T(8,128)(2,1)S(1)}, bf16[1,256,2048]{2,1,0:T(8,128)(2,1)S(1)}, u32[]{:S(2)}, u32[]{:S(2)}) %collective-permute-start.9) | collective-permute-done | bytes 1048608 | tf_op jit(solution)/shard_map/ppermute | solution.py:13
  238.9 14.0 %multiply_convert_fusion.2 = (bf16[1,256,2048]{2,1,0:T(8,128)(2,1)}, f32[1,256,2048]{2,1,0:T(8,128)}, bf16[1,256,2048]{2,1,0:T(8,128)(2,1)}) fusion(f32[2048]{0:T(1024)S(1)} %bitcast.194, f32[2048]{0:T(1024)S(1)} %bitcast.93, f32[2048]{0:T(1024)S(1)} %get-tuple-element.146, f32[2048]{0:T(1024)S(1)} %bitcast.197, f32[2048]{0:T(1024)S(1)} %get-tuple-element.147, ...), kind=kLoop, calls=%fused_computation.308 | loop fusion | flops 74973184 | bytes 25324032 | tf_op jit(solution)/shard_map/convert_element_type | solution.py:96
  253.4 11.1 %fusion.97 = (bf16[1,256,2048]{2,1,0:T(8,128)(2,1)S(1)}, f32[1,256,2048]{2,1,0:T(8,128)S(1)}) fusion(f32[2048]{0:T(1024)} %bitcast.192, f32[2048]{0:T(1024)S(1)} %bitcast.116, f32[2048]{0:T(1024)} %bitcast.145, pred[256]{0:T(512)(128)(4,1)} %get-tuple-element.134, f32[2048]{0:T(1024)} %bitcast.189, f32[2048]{0:T(1024)} %bitcast.198, f32[2048]{0:T(1024)} %bitcast.128, ...), kind=kOutput, calls=%fused_computation.216 | convolution fusion | flops 4315414528 | bytes 24183040 | tf_op jit(solution)/shard_map/bro,oc->brc/dot_general | solution.py:104
  265.8 22.3 %collective-permute-done.10 = bf16[1,256,2048]{2,1,0:T(8,128)(2,1)S(1)} collective-permute-done((bf16[1,256,2048]{2,1,0:T(8,128)(2,1)S(1)}, bf16[1,256,2048]{2,1,0:T(8,128)(2,1)S(1)}, u32[]{:S(2)}, u32[]{:S(2)}) %collective-permute-start.10) | collective-permute-done | bytes 1048608 | tf_op jit(solution)/shard_map/ppermute | solution.py:13
  288.2 7.5 %fusion.82 = (f32[2048]{0:T(1024)}, f32[2048]{0:T(1024)}, f32[2048]{0:T(1024)}, f32[2048]{0:T(1024)}, f32[2048]{0:T(1024)}, /*index=5*/f32[2048]{0:T(1024)}, f32...) fusion(bf16[1,256,2048]{2,1,0:T(8,128)(2,1)S(1)} %copy-done.47,, ...), kind=kLoop, calls=%fused_computation.201 | loop fusion | flops 47667200 | bytes 9691648 | tf_op jit(solution)/shard_map/reduce_sum | solution.py:129
  297.5 95.6 %collective-permute-done.11 = bf16[1,256,2048]{2,1,0:T(8,128)(2,1)S(1)} collective-permute-done((bf16[1,256,2048]{2,1,0:T(8,128)(2,1)S(1)}, bf16[1,256,2048]{2,1,0:T(8,128)(2,1)S(1)}, u32[]{:S(2)}, u32[]{:S(2)}) %collective-permute-start.11) | collective-permute-done | bytes 1048608 | tf_op jit(solution)/shard_map/ppermute | solution.py:13
  393.2 1.5 fusion.114
  395.3 13.4 %collective-permute-start.12 = (bf16[1,128,2048]{2,1,0:T(8,128)(2,1)S(1)}, bf16[1,128,2048]{2,1,0:T(8,128)(2,1)S(1)}, u32[]{:S(2)}, u32[]{:S(2)}) collective-permute-start(bf16[1,128,2048]{2,1,0:T(8,128)(2,1)S(1)} %get-tuple-element.112), channel_id=1, source_target_pairs={{4,0},{8,4},{12,8},{5,1},{9,5},{13,9},{6,2},{10,6},{14,10},{7,3},{... | collective-permute-start | bytes 1572872 | tf_op jit(solution)/shard_map/ppermute | solution.py:13
  408.8 9.2 %collective-permute-done.12 = bf16[1,128,2048]{2,1,0:T(8,128)(2,1)S(1)} collective-permute-done((bf16[1,128,2048]{2,1,0:T(8,128)(2,1)S(1)}, bf16[1,128,2048]{2,1,0:T(8,128)(2,1)S(1)}, u32[]{:S(2)}, u32[]{:S(2)}) %collective-permute-start.12) | collective-permute-done | bytes 524320 | tf_op jit(solution)/shard_map/ppermute | solution.py:13
  418.0 1.5 fusion.122
  420.1 1.4 collective-permute-start.13
  421.6 7.7 %collective-permute-done.13 = bf16[1,64,2048]{2,1,0:T(8,128)(2,1)S(1)} collective-permute-done((bf16[1,64,2048]{2,1,0:T(8,128)(2,1)S(1)}, bf16[1,64,2048]{2,1,0:T(8,128)(2,1)S(1)}, u32[]{:S(2)}, u32[]{:S(2)}) %collective-permute-start.13) | collective-permute-done | bytes 262176 | tf_op jit(solution)/shard_map/ppermute | solution.py:13
  429.3 1.5 fusion.130
  431.3 1.4 collective-permute-start.14
  432.9 5.5 %collective-permute-done.14 = bf16[1,32,2048]{2,1,0:T(8,128)(2,1)S(1)} collective-permute-done((bf16[1,32,2048]{2,1,0:T(8,128)(2,1)S(1)}, bf16[1,32,2048]{2,1,0:T(8,128)(2,1)S(1)}, u32[]{:S(2)}, u32[]{:S(2)}) %collective-permute-start.14) | collective-permute-done | bytes 131104 | tf_op jit(solution)/shard_map/ppermute | solution.py:13
  438.4 1.5 fusion.138
  439.9 4.0 fusion.53
  446.1 12.0 %fusion.2 = bf16[1,256,4096]{2,1,0:T(8,128)(2,1)} fusion(bf16[4096,2048]{1,0:T(8,128)(2,1)} %param.12, bf16[1,256,2048]{2,1,0:T(8,128)(2,1)} %get-tuple-element.102), kind=kOutput, calls=%fused_computation.3 | convolution fusion | flops 4296015872 | bytes 19922944 | tf_op jit(solution)/shard_map/brc,oc->bro/dot_general | solution.py:97
  459.7 1.6 fusion.134
  461.4 10.1 %multiply_convert_fusion = bf16[512,2048]{1,0:T(8,128)(2,1)} fusion(bf16[1,2048,2048]{2,1,0:T(8,128)(2,1)} %all-gather.5.cloned.1.call-done, bf16[1,2048,512]{2,1,0:T(8,128)(2,1)} %bitcast.126), kind=kOutput, calls=%fused_computation.4 | convolution fusion | flops 4297064448 | bytes 12582912 | tf_op jit(solution)/shard_map/bto,bti->oi/dot_general | solution.py:107
  471.5 3.8 fusion.48
  475.4 1.5 collective-permute-start.16
  477.1 5.0 collective-permute-done.16
  483.2 4.2 fusion.58
  489.1 4.1 collective-permute-done.17
  494.8 1.4 collective-permute-start.18
  496.5 4.0 collective-permute-done.18
  500.5 2.0 fusion.170
  502.9 7.2 %fusion.38 = (f32[2048]{0:T(1024)}, f32[2048]{0:T(1024)S(1)}, f32[2048]{0:T(1024)}, f32[2048]{0:T(1024)}, f32[2048]{0:T(1024)}, /*index=5*/f32[2048]{0:T(1024)},...) fusion(f32[1,256,2048]{2,1,0:T(8,128)S(1)} %get-tuple-element.145, ...), kind=kLoop, calls=%fused_computation.157 | loop fusion | flops 25149440 | bytes 11641344 | tf_op jit(solution)/shard_map/reduce_sum | solution.py:130
  514.0 1.4 collective-permute-done.20
  515.4 2.1 collective-permute-start.21
  519.8 2.9 collective-permute-done.21
  522.8 2.6 collective-permute-start.22
  525.4 1.7 add_convert_fusion
  527.2 7.2 %collective-permute-done.22 = f32[17,2048]{1,0:T(8,128)S(1)} collective-permute-done((f32[17,2048]{1,0:T(8,128)S(1)}, f32[17,2048]{1,0:T(8,128)S(1)}, u32[]{:S(2)}, u32[]{:S(2)}) %collective-permute-start.22) | collective-permute-done | bytes 139296 | tf_op jit(solution)/shard_map/ppermute | solution.py:25
  (404 shorter events, 33.1 us)
Async XLA Ops:
  7.2 39.3 %all-gather.3.cloned.1.call-start = ((), (), s32[]{:S(2)}) async-start(), calls=%async_computation.2 | async-start | bytes 3145728 | tf_op jit(solution)/shard_map/all_gather | solution.py:62
  8.0 8.0 %collective-permute-start = (bf16[1,1,2048]{2,1,0:T(2,128)(2,1)S(1)}, bf16[1,1,2048]{2,1,0:T(2,128)(2,1)S(1)}, u32[]{:S(2)}, u32[]{:S(2)}) collective-permute-start(bf16[1,1,2048]{2,1,0:T(2,128)(2,1)S(1)} %slice.106), channel_id=1, source_target_pairs={{0,4},{4,8},{8,12},{1,5},{5,9},{9,13},{2,6},{6,10},{10,14},{3,7},{... | collective-permute-start | bytes 12296 | tf_op jit(solution)/shard_map/ppermute | solution.py:13
  16.0 74.4 %copy-start.156 = (pred[256]{0:T(512)(128)(4,1)}, pred[256]{0:T(512)(128)(4,1)S(1)}, u32[]{:S(2)}) copy-start(pred[256]{0:T(512)(128)(4,1)S(1)} %get-tuple-element.140) | copy-start | bytes 772
  16.0 110.6 %copy-start.148 = (pred[256]{0:T(512)(128)(4,1)}, pred[256]{0:T(512)(128)(4,1)S(1)}, u32[]{:S(2)}) copy-start(pred[256]{0:T(512)(128)(4,1)S(1)} %get-tuple-element.139) | copy-start | bytes 772
  16.0 128.7 %copy-start.131 = (pred[256]{0:T(512)(128)(4,1)}, pred[256]{0:T(512)(128)(4,1)S(1)}, u32[]{:S(2)}) copy-start(pred[256]{0:T(512)(128)(4,1)S(1)} %get-tuple-element.138) | copy-start | bytes 772
  18.3 220.5 %copy-start = (bf16[1,256,2048]{2,1,0:T(8,128)(2,1)}, bf16[1,256,2048]{2,1,0:T(8,128)(2,1)S(1)}, u32[]{:S(2)}) copy-start(bf16[1,256,2048]{2,1,0:T(8,128)(2,1)S(1)} %fusion.33) | copy-start | bytes 3145732
  18.3 4.8 collective-permute-start.1
  23.9 5.6 %collective-permute-start.2 = (bf16[1,4,2048]{2,1,0:T(4,128)(2,1)S(1)}, bf16[1,4,2048]{2,1,0:T(4,128)(2,1)S(1)}, u32[]{:S(2)}, u32[]{:S(2)}) collective-permute-start(bf16[1,4,2048]{2,1,0:T(4,128)(2,1)S(1)} %slice.158), channel_id=1, source_target_pairs={{0,4},{4,8},{8,12},{1,5},{5,9},{9,13},{2,6},{6,10},{10,14},{3,7},{... | collective-permute-start | bytes 49160 | tf_op jit(solution)/shard_map/ppermute | solution.py:13
  30.3 60.1 %copy-start.4 = (bf16[1,256,2048]{2,1,0:T(8,128)(2,1)}, bf16[1,256,2048]{2,1,0:T(8,128)(2,1)S(1)}, u32[]{:S(2)}) copy-start(bf16[1,256,2048]{2,1,0:T(8,128)(2,1)S(1)} %fusion.42) | copy-start | bytes 3145732
  30.3 60.0 %collective-permute-start.3 = (bf16[1,8,2048]{2,1,0:T(8,128)(2,1)S(1)}, bf16[1,8,2048]{2,1,0:T(8,128)(2,1)S(1)}, u32[]{:S(2)}, u32[]{:S(2)}) collective-permute-start(bf16[1,8,2048]{2,1,0:T(8,128)(2,1)S(1)} %slice.160), channel_id=1, source_target_pairs={{0,4},{4,8},{8,12},{1,5},{5,9},{9,13},{2,6},{6,10},{10,14},{3,7},{... | collective-permute-start | bytes 98312 | tf_op jit(solution)/shard_map/ppermute | solution.py:13
  85.7 86.0 %all-to-all-start = ((bf16[8,2,65536]{2,1,0:T(2,128)(2,1)}), bf16[8,2,65536]{2,1,0:T(2,128)(2,1)}, u32[]{:S(2)}, u32[]{:S(2)}) async-start(bf16[8,2,65536]{2,1,0:T(2,128)(2,1)} %reshape.2423), calls=%async_computation | async-start | bytes 4194304 | tf_op jit(solution)/shard_map/all_to_all | solution.py:63
  90.3 371.0 %all-gather.5.cloned.1.call-start = ((), (), s32[]{:S(2)}) async-start(), calls=%async_computation.4 | async-start | bytes 9437184 | tf_op jit(solution)/shard_map/all_gather | solution.py:105
  92.1 35.0 %copy-start.12 = (bf16[1,256,2048]{2,1,0:T(8,128)(2,1)}, bf16[1,256,2048]{2,1,0:T(8,128)(2,1)S(1)}, u32[]{:S(2)}) copy-start(bf16[1,256,2048]{2,1,0:T(8,128)(2,1)S(1)} %fusion.47) | copy-start | bytes 3145732
  92.1 34.4 %collective-permute-start.4 = (bf16[1,16,2048]{2,1,0:T(8,128)(2,1)S(1)}, bf16[1,16,2048]{2,1,0:T(8,128)(2,1)S(1)}, u32[]{:S(2)}, u32[]{:S(2)}) collective-permute-start(bf16[1,16,2048]{2,1,0:T(8,128)(2,1)S(1)} %slice.162), channel_id=1, source_target_pairs={{0,4},{4,8},{8,12},{1,5},{5,9},{9,13},{2,6},{6,10},{10,14},{3,7},{... | collective-permute-start | bytes 196616 | tf_op jit(solution)/shard_map/ppermute | solution.py:13
  96.1 45.7 %copy-start.16 = (bf16[1,240,2048]{2,1,0:T(8,128)(2,1)}, bf16[1,240,2048]{2,1,0:T(8,128)(2,1)S(1)}, u32[]{:S(2)}) copy-start(bf16[1,240,2048]{2,1,0:T(8,128)(2,1)S(1)} %slice.163) | copy-start | bytes 2949124
  127.2 17.5 %collective-permute-start.5 = (bf16[1,32,2048]{2,1,0:T(8,128)(2,1)S(1)}, bf16[1,32,2048]{2,1,0:T(8,128)(2,1)S(1)}, u32[]{:S(2)}, u32[]{:S(2)}) collective-permute-start(bf16[1,32,2048]{2,1,0:T(8,128)(2,1)S(1)} %slice.164), channel_id=1, source_target_pairs={{0,4},{4,8},{8,12},{1,5},{5,9},{9,13},{2,6},{6,10},{10,14},{3,7},{... | collective-permute-start | bytes 393224 | tf_op jit(solution)/shard_map/ppermute | solution.py:13
  145.3 9.3 %collective-permute-start.6 = (bf16[1,64,2048]{2,1,0:T(8,128)(2,1)S(1)}, bf16[1,64,2048]{2,1,0:T(8,128)(2,1)S(1)}, u32[]{:S(2)}, u32[]{:S(2)}) collective-permute-start(bf16[1,64,2048]{2,1,0:T(8,128)(2,1)S(1)} %slice.166), channel_id=1, source_target_pairs={{0,4},{4,8},{8,12},{1,5},{5,9},{9,13},{2,6},{6,10},{10,14},{3,7},{... | collective-permute-start | bytes 786440 | tf_op jit(solution)/shard_map/ppermute | solution.py:13
  155.3 14.0 %collective-permute-start.7 = (bf16[1,128,2048]{2,1,0:T(8,128)(2,1)S(1)}, bf16[1,128,2048]{2,1,0:T(8,128)(2,1)S(1)}, u32[]{:S(2)}, u32[]{:S(2)}) collective-permute-start(bf16[1,128,2048]{2,1,0:T(8,128)(2,1)S(1)} %get-tuple-element.113), channel_id=1, source_target_pairs={{0,4},{4,8},{8,12},{1,5},{5,9},{9,13},{2,6},{6,10},{10,14},{3,7},{... | collective-permute-start | bytes 1572872 | tf_op jit(solution)/shard_map/ppermute | solution.py:13
  186.2 52.5 %copy-start.2 = (bf16[1,256,2048]{2,1,0:T(8,128)(2,1)S(1)}, bf16[1,256,2048]{2,1,0:T(8,128)(2,1)}, u32[]{:S(2)}) copy-start(bf16[1,256,2048]{2,1,0:T(8,128)(2,1)} %param.7) | copy-start | bytes 3145732
  186.2 52.5 %copy-start.5 = (bf16[1,256,2048]{2,1,0:T(8,128)(2,1)S(1)}, bf16[1,256,2048]{2,1,0:T(8,128)(2,1)}, u32[]{:S(2)}) copy-start(bf16[1,256,2048]{2,1,0:T(8,128)(2,1)} %copy-done.4) | copy-start | bytes 3145732
  186.2 52.5 %copy-start.8 = (bf16[1,256,2048]{2,1,0:T(8,128)(2,1)S(1)}, bf16[1,256,2048]{2,1,0:T(8,128)(2,1)}, u32[]{:S(2)}) copy-start(bf16[1,256,2048]{2,1,0:T(8,128)(2,1)} %copy-done.7) | copy-start | bytes 3145732
  186.2 52.5 %copy-start.57 = (bf16[1,16,2048]{2,1,0:T(8,128)(2,1)S(1)}, bf16[1,16,2048]{2,1,0:T(8,128)(2,1)}, u32[]{:S(2)}) copy-start(bf16[1,16,2048]{2,1,0:T(8,128)(2,1)} %copy-done.56) | copy-start | bytes 196612
  186.3 52.5 %copy-start.60 = (bf16[1,8,2048]{2,1,0:T(8,128)(2,1)S(1)}, bf16[1,8,2048]{2,1,0:T(8,128)(2,1)}, u32[]{:S(2)}) copy-start(bf16[1,8,2048]{2,1,0:T(8,128)(2,1)} %copy-done.59) | copy-start | bytes 98308
  186.3 52.5 %copy-start.63 = (bf16[1,4,2048]{2,1,0:T(4,128)(2,1)S(1)}, bf16[1,4,2048]{2,1,0:T(4,128)(2,1)}, u32[]{:S(2)}) copy-start(bf16[1,4,2048]{2,1,0:T(4,128)(2,1)} %copy-done.62) | copy-start | bytes 49156
  186.3 52.5 %copy-start.80 = (bf16[1,1,2048]{2,1,0:T(2,128)(2,1)S(1)}, bf16[1,1,2048]{2,1,0:T(2,128)(2,1)}, u32[]{:S(2)}) copy-start(bf16[1,1,2048]{2,1,0:T(2,128)(2,1)} %copy-done.79) | copy-start | bytes 12292
  186.3 52.5 %copy-start.83 = (bf16[1,2,2048]{2,1,0:T(2,128)(2,1)S(1)}, bf16[1,2,2048]{2,1,0:T(2,128)(2,1)}, u32[]{:S(2)}) copy-start(bf16[1,2,2048]{2,1,0:T(2,128)(2,1)} %copy-done.82) | copy-start | bytes 24580
  186.3 52.5 %copy-start.132 = (pred[256]{0:T(512)(128)(4,1)S(1)}, pred[256]{0:T(512)(128)(4,1)}, u32[]{:S(2)}) copy-start(pred[256]{0:T(512)(128)(4,1)} %copy-done.131) | copy-start | bytes 772
  186.3 52.5 %copy-start.136 = (pred[256]{0:T(512)(128)(4,1)S(1)}, pred[256]{0:T(512)(128)(4,1)}, u32[]{:S(2)}) copy-start(pred[256]{0:T(512)(128)(4,1)} %get-tuple-element.136) | copy-start | bytes 772
  186.3 52.5 %copy-start.140 = (pred[256]{0:T(512)(128)(4,1)S(1)}, pred[256]{0:T(512)(128)(4,1)}, u32[]{:S(2)}) copy-start(pred[256]{0:T(512)(128)(4,1)} %get-tuple-element.137) | copy-start | bytes 772
  186.3 52.5 %copy-start.143 = (pred[256]{0:T(512)(128)(4,1)S(1)}, pred[256]{0:T(512)(128)(4,1)}, u32[]{:S(2)}) copy-start(pred[256]{0:T(512)(128)(4,1)} %copy-done.142) | copy-start | bytes 772
  186.3 52.5 %copy-start.146 = (pred[256]{0:T(512)(128)(4,1)S(1)}, pred[256]{0:T(512)(128)(4,1)}, u32[]{:S(2)}) copy-start(pred[256]{0:T(512)(128)(4,1)} %copy-done.145) | copy-start | bytes 772
  186.3 52.5 %copy-start.149 = (pred[256]{0:T(512)(128)(4,1)S(1)}, pred[256]{0:T(512)(128)(4,1)}, u32[]{:S(2)}) copy-start(pred[256]{0:T(512)(128)(4,1)} %copy-done.148) | copy-start | bytes 772
  186.4 52.5 %copy-start.151 = (pred[256]{0:T(512)(128)(4,1)S(1)}, pred[256]{0:T(512)(128)(4,1)}, u32[]{:S(2)}) copy-start(pred[256]{0:T(512)(128)(4,1)} %get-tuple-element.135) | copy-start | bytes 772
  186.4 52.5 %copy-start.154 = (pred[256]{0:T(512)(128)(4,1)S(1)}, pred[256]{0:T(512)(128)(4,1)}, u32[]{:S(2)}) copy-start(pred[256]{0:T(512)(128)(4,1)} %copy-done.153) | copy-start | bytes 772
  186.4 52.5 %copy-start.157 = (pred[256]{0:T(512)(128)(4,1)S(1)}, pred[256]{0:T(512)(128)(4,1)}, u32[]{:S(2)}) copy-start(pred[256]{0:T(512)(128)(4,1)} %copy-done.156) | copy-start | bytes 772
  186.4 52.5 %copy-start.159 = (pred[256]{0:T(512)(128)(4,1)S(1)}, pred[256]{0:T(512)(128)(4,1)}, u32[]{:S(2)}) copy-start(pred[256]{0:T(512)(128)(4,1)} %get-tuple-element.134) | copy-start | bytes 772
  186.4 24.9 %collective-permute-start.8 = (bf16[1,256,2048]{2,1,0:T(8,128)(2,1)}, bf16[1,256,2048]{2,1,0:T(8,128)(2,1)S(1)}, u32[]{:S(2)}, u32[]{:S(2)}) collective-permute-start(bf16[1,256,2048]{2,1,0:T(8,128)(2,1)} %fusion.67), channel_id=1, source_target_pairs={{0,4},{4,8},{8,12},{1,5},{5,9},{9,13},{2,6},{6,10},{10,14},{3,7},{... | collective-permute-start | bytes 3145736 | tf_op jit(solution)/shard_map/ppermute | solution.py:13
  211.3 41.6 %copy-start.34 = (bf16[1,256,2048]{2,1,0:T(8,128)(2,1)}, bf16[1,256,2048]{2,1,0:T(8,128)(2,1)S(1)}, u32[]{:S(2)}) copy-start(bf16[1,256,2048]{2,1,0:T(8,128)(2,1)S(1)} %collective-permute-done.8) | copy-start | bytes 3145732
  213.5 39.5 %copy-start.36 = (bf16[1,256,2048]{2,1,0:T(8,128)(2,1)}, bf16[1,256,2048]{2,1,0:T(8,128)(2,1)S(1)}, u32[]{:S(2)}) copy-start(bf16[1,256,2048]{2,1,0:T(8,128)(2,1)S(1)} %fusion.17) | copy-start | bytes 3145732
  213.5 25.3 %collective-permute-start.9 = (bf16[1,256,2048]{2,1,0:T(8,128)(2,1)S(1)}, bf16[1,256,2048]{2,1,0:T(8,128)(2,1)S(1)}, u32[]{:S(2)}, u32[]{:S(2)}) collective-permute-start(bf16[1,256,2048]{2,1,0:T(8,128)(2,1)S(1)} %fusion.17), channel_id=1, source_target_pairs={{0,8},{4,12},{1,9},{5,13},{2,10},{6,14},{3,11},{7,15},{16,24},{20,... | collective-permute-start | bytes 3145736 | tf_op jit(solution)/shard_map/ppermute | solution.py:13
  253.2 249.4 %reduce-scatter.2.cloned.1.call-start = ((), (), s32[]{:S(2)}) async-start(), calls=%async_computation.3 | async-start | bytes 3145728 | tf_op jit(solution)/shard_map/reduce_scatter | solution.py:100
  253.2 34.9 %copy-start.27 = (bf16[1,256,2048]{2,1,0:T(8,128)(2,1)S(1)}, bf16[1,256,2048]{2,1,0:T(8,128)(2,1)}, u32[]{:S(2)}) copy-start(bf16[1,256,2048]{2,1,0:T(8,128)(2,1)} %fusion.67) | copy-start | bytes 3145732
  253.2 34.9 %copy-start.35 = (bf16[1,256,2048]{2,1,0:T(8,128)(2,1)S(1)}, bf16[1,256,2048]{2,1,0:T(8,128)(2,1)}, u32[]{:S(2)}) copy-start(bf16[1,256,2048]{2,1,0:T(8,128)(2,1)} %copy-done.34) | copy-start | bytes 3145732
  253.2 34.9 %copy-start.37 = (bf16[1,256,2048]{2,1,0:T(8,128)(2,1)S(1)}, bf16[1,256,2048]{2,1,0:T(8,128)(2,1)}, u32[]{:S(2)}) copy-start(bf16[1,256,2048]{2,1,0:T(8,128)(2,1)} %copy-done.36) | copy-start | bytes 3145732
  253.3 34.9 %copy-start.46 = (bf16[1,256,2048]{2,1,0:T(8,128)(2,1)S(1)}, bf16[1,256,2048]{2,1,0:T(8,128)(2,1)}, u32[]{:S(2)}) copy-start(bf16[1,256,2048]{2,1,0:T(8,128)(2,1)} %copy-done.45) | copy-start | bytes 3145732
  253.3 34.9 %copy-start.47 = (bf16[1,256,2048]{2,1,0:T(8,128)(2,1)S(1)}, bf16[1,256,2048]{2,1,0:T(8,128)(2,1)}, u32[]{:S(2)}) copy-start(bf16[1,256,2048]{2,1,0:T(8,128)(2,1)} %get-tuple-element.104) | copy-start | bytes 3145732
  253.3 34.9 %copy-start.51 = (f32[1,2048]{1,0:T(1,128)S(1)}, f32[1,2048]{1,0:T(1,128)}, u32[]{:S(2)}) copy-start(f32[1,2048]{1,0:T(1,128)} %copy-done.50) | copy-start | bytes 24580
  264.5 23.6 %collective-permute-start.10 = (bf16[1,256,2048]{2,1,0:T(8,128)(2,1)S(1)}, bf16[1,256,2048]{2,1,0:T(8,128)(2,1)S(1)}, u32[]{:S(2)}, u32[]{:S(2)}) collective-permute-start(bf16[1,256,2048]{2,1,0:T(8,128)(2,1)S(1)} %get-tuple-element.144), channel_id=1, source_target_pairs={{8,0},{12,4},{9,1},{13,5},{10,2},{14,6},{11,3},{15,7},{24,16},{28,... | collective-permute-start | bytes 3145736 | tf_op jit(solution)/shard_map/ppermute | solution.py:13
  295.7 97.4 %copy-start.31 = (bf16[1,128,2048]{2,1,0:T(8,128)(2,1)S(1)}, bf16[1,128,2048]{2,1,0:T(8,128)(2,1)}, u32[]{:S(2)}) copy-start(bf16[1,128,2048]{2,1,0:T(8,128)(2,1)} %copy-done.30) | copy-start | bytes 1572868
  295.7 97.4 %copy-start.42 = (bf16[1,128,2048]{2,1,0:T(8,128)(2,1)S(1)}, bf16[1,128,2048]{2,1,0:T(8,128)(2,1)}, u32[]{:S(2)}) copy-start(bf16[1,128,2048]{2,1,0:T(8,128)(2,1)} %copy-done.41) | copy-start | bytes 1572868
  295.7 97.4 %copy-start.137 = (pred[256]{0:T(512)(128)(4,1)S(1)}, pred[256]{0:T(512)(128)(4,1)}, u32[]{:S(2)}) copy-start(pred[256]{0:T(512)(128)(4,1)} %get-tuple-element.136) | copy-start | bytes 772
  296.2 98.5 %copy-start.66 = (f32[1,2048]{1,0:T(1,128)S(1)}, f32[1,2048]{1,0:T(1,128)}, u32[]{:S(2)}) copy-start(f32[1,2048]{1,0:T(1,128)} %copy-done.65) | copy-start | bytes 24580
  296.2 96.9 %collective-permute-start.11 = (bf16[1,256,2048]{2,1,0:T(8,128)(2,1)S(1)}, bf16[1,256,2048]{2,1,0:T(8,128)(2,1)S(1)}, u32[]{:S(2)}, u32[]{:S(2)}) collective-permute-start(bf16[1,256,2048]{2,1,0:T(8,128)(2,1)S(1)} %fusion.105), channel_id=1, source_target_pairs={{4,0},{8,4},{12,8},{5,1},{9,5},{13,9},{6,2},{10,6},{14,10},{7,3},{... | collective-permute-start | bytes 3145736 | tf_op jit(solution)/shard_map/ppermute | solution.py:13
  395.3 22.7 %collective-permute-start.12 = (bf16[1,128,2048]{2,1,0:T(8,128)(2,1)S(1)}, bf16[1,128,2048]{2,1,0:T(8,128)(2,1)S(1)}, u32[]{:S(2)}, u32[]{:S(2)}) collective-permute-start(bf16[1,128,2048]{2,1,0:T(8,128)(2,1)S(1)} %get-tuple-element.112), channel_id=1, source_target_pairs={{4,0},{8,4},{12,8},{5,1},{9,5},{13,9},{6,2},{10,6},{14,10},{7,3},{... | collective-permute-start | bytes 1572872 | tf_op jit(solution)/shard_map/ppermute | solution.py:13
  420.1 9.2 %collective-permute-start.13 = (bf16[1,64,2048]{2,1,0:T(8,128)(2,1)S(1)}, bf16[1,64,2048]{2,1,0:T(8,128)(2,1)S(1)}, u32[]{:S(2)}, u32[]{:S(2)}) collective-permute-start(bf16[1,64,2048]{2,1,0:T(8,128)(2,1)S(1)} %slice.173), channel_id=1, source_target_pairs={{4,0},{8,4},{12,8},{5,1},{9,5},{13,9},{6,2},{10,6},{14,10},{7,3},{... | collective-permute-start | bytes 786440 | tf_op jit(solution)/shard_map/ppermute | solution.py:13
  431.3 7.0 %collective-permute-start.14 = (bf16[1,32,2048]{2,1,0:T(8,128)(2,1)S(1)}, bf16[1,32,2048]{2,1,0:T(8,128)(2,1)S(1)}, u32[]{:S(2)}, u32[]{:S(2)}) collective-permute-start(bf16[1,32,2048]{2,1,0:T(8,128)(2,1)S(1)} %slice.175), channel_id=1, source_target_pairs={{4,0},{8,4},{12,8},{5,1},{9,5},{13,9},{6,2},{10,6},{14,10},{7,3},{... | collective-permute-start | bytes 393224 | tf_op jit(solution)/shard_map/ppermute | solution.py:13
  444.9 14.7 %collective-permute-start.15 = (bf16[1,16,2048]{2,1,0:T(8,128)(2,1)S(1)}, bf16[1,16,2048]{2,1,0:T(8,128)(2,1)S(1)}, u32[]{:S(2)}, u32[]{:S(2)}) collective-permute-start(bf16[1,16,2048]{2,1,0:T(8,128)(2,1)S(1)} %slice.354), channel_id=1, source_target_pairs={{4,0},{8,4},{12,8},{5,1},{9,5},{13,9},{6,2},{10,6},{14,10},{7,3},{... | collective-permute-start | bytes 196616 | tf_op jit(solution)/shard_map/ppermute | solution.py:13
  475.4 6.6 %collective-permute-start.16 = (bf16[1,8,2048]{2,1,0:T(8,128)(2,1)S(1)}, bf16[1,8,2048]{2,1,0:T(8,128)(2,1)S(1)}, u32[]{:S(2)}, u32[]{:S(2)}) collective-permute-start(bf16[1,8,2048]{2,1,0:T(8,128)(2,1)S(1)} %slice.356), channel_id=1, source_target_pairs={{4,0},{8,4},{12,8},{5,1},{9,5},{13,9},{6,2},{10,6},{14,10},{7,3},{... | collective-permute-start | bytes 98312 | tf_op jit(solution)/shard_map/ppermute | solution.py:13
  487.4 5.8 %collective-permute-start.17 = (bf16[1,4,2048]{2,1,0:T(4,128)(2,1)S(1)}, bf16[1,4,2048]{2,1,0:T(4,128)(2,1)S(1)}, u32[]{:S(2)}, u32[]{:S(2)}) collective-permute-start(bf16[1,4,2048]{2,1,0:T(4,128)(2,1)S(1)} %slice.358), channel_id=1, source_target_pairs={{4,0},{8,4},{12,8},{5,1},{9,5},{13,9},{6,2},{10,6},{14,10},{7,3},{... | collective-permute-start | bytes 49160 | tf_op jit(solution)/shard_map/ppermute | solution.py:13
  494.8 5.7 %collective-permute-start.18 = (bf16[1,2,2048]{2,1,0:T(2,128)(2,1)S(1)}, bf16[1,2,2048]{2,1,0:T(2,128)(2,1)S(1)}, u32[]{:S(2)}, u32[]{:S(2)}) collective-permute-start(bf16[1,2,2048]{2,1,0:T(2,128)(2,1)S(1)} %slice.360), channel_id=1, source_target_pairs={{4,0},{8,4},{12,8},{5,1},{9,5},{13,9},{6,2},{10,6},{14,10},{7,3},{... | collective-permute-start | bytes 24584 | tf_op jit(solution)/shard_map/ppermute | solution.py:13
  513.9 1.5 collective-permute-start.20
  515.4 7.3 %collective-permute-start.21 = (f32[17,2048]{1,0:T(8,128)S(1)}, f32[17,2048]{1,0:T(8,128)S(1)}, u32[]{:S(2)}, u32[]{:S(2)}) collective-permute-start(f32[17,2048]{1,0:T(8,128)S(1)} %fusion.177), channel_id=1, source_target_pairs={{0,4},{4,0},{8,12},{12,8},{1,5},{5,1},{9,13},{13,9},{2,6},{6,2},{1... | collective-permute-start | bytes 417800 | tf_op jit(solution)/shard_map/ppermute | solution.py:25
  518.3 7.1 %collective-permute-start.19 = (bf16[1,1,2048]{2,1,0:T(2,128)(2,1)S(1)}, bf16[1,1,2048]{2,1,0:T(2,128)(2,1)S(1)}, u32[]{:S(2)}, u32[]{:S(2)}) collective-permute-start(bf16[1,1,2048]{2,1,0:T(2,128)(2,1)S(1)} %slice.362), channel_id=1, source_target_pairs={{4,0},{8,4},{12,8},{5,1},{9,5},{13,9},{6,2},{10,6},{14,10},{7,3},{... | collective-permute-start | bytes 12296 | tf_op jit(solution)/shard_map/ppermute | solution.py:13
  522.8 11.6 %collective-permute-start.22 = (f32[17,2048]{1,0:T(8,128)S(1)}, f32[17,2048]{1,0:T(8,128)S(1)}, u32[]{:S(2)}, u32[]{:S(2)}) collective-permute-start(f32[17,2048]{1,0:T(8,128)S(1)} %add.973), channel_id=1, source_target_pairs={{0,8},{4,12},{8,0},{12,4},{1,9},{5,13},{9,1},{13,5},{2,10},{6,14},... | collective-permute-start | bytes 417800 | tf_op jit(solution)/shard_map/ppermute | solution.py:25
  (124 other events, 1691.4 us)
Sparse Core Ops, SparseCore 0:
  13.1 33.3 all-gather.2
  253.3 135.8 all-gather.4
  458.3 33.7 reduce-scatter.1
